TPU v7x, 256 devices: a whole 4x4x8 slice. The times are simulated.
256 devices in a mesh: section: 8 (over y, core), seq: 8 (over z), chan: 4 (over x).
Axes of the slice: x: 4, y: 4, z: 8, core: 2. Of those that a mesh axis runs over, the one named last changes fastest.
Arguments:
- layer_rows: bfloat16 [8, 8192, 8192], P('section', 'seq', 'chan'), may hold values from -6 to 6
- in_weight: bfloat16 [8, 8192, 768], P('section', 'chan'), may hold values from -0.0625 to 0.0625
- long_filter: float32 [8, 8192, 256], P('section', ('seq', 'chan')), may hold values from -2 to 2, as said below
- skip_gain: float32 [8, 256], P('section'), may hold values from -4 to 4
Outputs:
- gated_out: bfloat16 [8, 8192, 256], P('section', ('seq', 'chan'))
Inputs may be any that keep to these rules, and one draw needn't show every extreme that they name: `long_filter`: filter taps of each channel.
All inputs are finite; a program needn't handle non-finite values.
Results may differ from a plain program's by a relative error of at most 0.0064.
Values may be sent and summed in bfloat16 or wider, within the bound.
No kernel may reach another device: no remote copies, remote signals or barrier semaphores. Data moves between devices by JAX's collectives and lax.ppermute only.
A program may use at most 64 MiB of HBM per device.

v0:
```python
import math

import jax
import jax.numpy as jnp
from jax import lax
from jax.sharding import PartitionSpec as P


def from_behind(value, axis, steps):
    count = lax.axis_size(axis)
    pairs = [(source, (source + steps) % count) for source in range(count)]
    return lax.ppermute(value, axis, pairs)


def transpose_blocks(data):
    return lax.all_to_all(data, ("seq", "chan"), split_axis=0, concat_axis=1, tiled=True)


def mix(table, data, form):
    return jnp.einsum(form, table, data, precision=lax.Precision.HIGHEST)


def body(layer_rows, in_weight, long_filter, skip_gain):
    chan_width = long_filter.shape[2]
    row_count = long_filter.shape[1]
    seq_devices = lax.axis_size(("seq", "chan"))
    block_rows = row_count // seq_devices
    fft_length = 2 * row_count * seq_devices
    device_index = lax.axis_index(("seq", "chan"))
    source = from_behind(layer_rows, "section", 1)
    picked = source[0]
    summed = lax.psum_scatter(
        jnp.dot(picked, in_weight[0], preferred_element_type=jnp.float32),
        "chan",
        scatter_dimension=0,
        tiled=True,
    )
    mixed = summed.astype(jnp.bfloat16)
    queries = mixed[:, :chan_width].astype(jnp.float32)
    key_part = mixed[:, chan_width : 2 * chan_width].astype(jnp.float32)
    values_part = mixed[:, 2 * chan_width :].astype(jnp.float32)
    signal = key_part * values_part
    coarse_freq = jnp.arange(2 * seq_devices, dtype=jnp.int32)
    block_ids = jnp.arange(seq_devices, dtype=jnp.int32)
    coarse_angle = (
        2.0
        * math.pi
        / (2 * seq_devices)
        * (coarse_freq[:, None] * block_ids[None, :] % (2 * seq_devices)).astype(jnp.float32)
    )
    coarse_cos = jnp.cos(coarse_angle)
    coarse_sin = jnp.sin(coarse_angle)
    positions = device_index * block_rows + jnp.arange(block_rows, dtype=jnp.int32)
    twist_angle = (
        2.0
        * math.pi
        / fft_length
        * (coarse_freq[:, None] * positions[None, :] % fft_length).astype(jnp.float32)
    )
    twist_cos = jnp.cos(twist_angle)[:, :, None]
    twist_sin = jnp.sin(twist_angle)[:, :, None]
    fine_ids = jnp.arange(row_count, dtype=jnp.int32)
    fine_angle = (
        2.0
        * math.pi
        / row_count
        * (fine_ids[:, None] * fine_ids[None, :] % row_count).astype(jnp.float32)
    )
    fine_cos = jnp.cos(fine_angle)
    fine_sin = jnp.sin(fine_angle)
    paired = jnp.concatenate([signal, long_filter[0]], axis=1)
    blocks = transpose_blocks(paired.reshape(seq_devices, 1, block_rows, 2 * chan_width))
    blocks = blocks.reshape(seq_devices, block_rows, 2 * chan_width)
    coarse_real = mix(coarse_cos, blocks, "km,mrc->krc")
    coarse_imag = -mix(coarse_sin, blocks, "km,mrc->krc")
    twist_real = coarse_real * twist_cos + coarse_imag * twist_sin
    twist_imag = coarse_imag * twist_cos - coarse_real * twist_sin
    packed = jnp.concatenate([twist_real, twist_imag], axis=2)
    arrived = transpose_blocks(packed.reshape(2 * seq_devices, 1, block_rows, 4 * chan_width))
    arrived = arrived.reshape(2, row_count, 4 * chan_width)
    inner_real = arrived[:, :, : 2 * chan_width]
    inner_imag = arrived[:, :, 2 * chan_width :]
    spec_real = mix(fine_cos, inner_real, "kr,jrc->jkc") + mix(fine_sin, inner_imag, "kr,jrc->jkc")
    spec_imag = mix(fine_cos, inner_imag, "kr,jrc->jkc") - mix(fine_sin, inner_real, "kr,jrc->jkc")
    sig_real = spec_real[:, :, :chan_width]
    sig_imag = spec_imag[:, :, :chan_width]
    fil_real = spec_real[:, :, chan_width:]
    fil_imag = spec_imag[:, :, chan_width:]
    prod_real = sig_real * fil_real - sig_imag * fil_imag
    prod_imag = sig_real * fil_imag + sig_imag * fil_real
    fine_cos3 = fine_cos.reshape(seq_devices, block_rows, row_count)
    fine_sin3 = fine_sin.reshape(seq_devices, block_rows, row_count)
    back_real = mix(fine_cos3, prod_real, "qpk,jkc->qjpc") - mix(
        fine_sin3, prod_imag, "qpk,jkc->qjpc"
    )
    back_imag = mix(fine_cos3, prod_imag, "qpk,jkc->qjpc") + mix(
        fine_sin3, prod_real, "qpk,jkc->qjpc"
    )
    returned = transpose_blocks(jnp.concatenate([back_real, back_imag], axis=3))
    returned = returned.reshape(2 * seq_devices, block_rows, 2 * chan_width)
    ret_real = returned[:, :, :chan_width]
    ret_imag = returned[:, :, chan_width:]
    untwist_real = ret_real * twist_cos - ret_imag * twist_sin
    untwist_imag = ret_imag * twist_cos + ret_real * twist_sin
    conv_blocks = (
        mix(coarse_cos, untwist_real, "km,krc->mrc") - mix(coarse_sin, untwist_imag, "km,krc->mrc")
    ) / fft_length
    conv = transpose_blocks(conv_blocks.reshape(seq_devices, 1, block_rows, chan_width))
    conv = conv.reshape(row_count, chan_width)
    gated_out = queries * (conv + skip_gain[0][None, :] * signal)
    return gated_out.astype(jnp.bfloat16)[None]


def solution(mesh):
    in_specs = (
        P("section", "seq", "chan"),
        P("section", "chan", None),
        P("section", ("seq", "chan"), None),
        P("section", None),
    )
    out_specs = P("section", ("seq", "chan"), None)
    return jax.shard_map(body, mesh=mesh, in_specs=in_specs, out_specs=out_specs, check_vma=False)
```

profile of v0, /device:TPU:8, one launch (start us, length us, event | category | flops | bytes accessed | tf_op | source)
XLA Modules:
  0.0 275.4 jit_solution(13743493784468213230)
XLA Ops:
  6.5 48.1 %collective-permute-done = bf16[1,1024,2048]{2,1,0:T(8,128)(2,1)S(1)} collective-permute-done((bf16[1,1024,2048]{2,1,0:T(8,128)(2,1)}, bf16[1,1024,2048]{2,1,0:T(8,128)(2,1)S(1)}, u32[]{:S(2)}, u32[]{:S(2)}) %collective-permute-start) | collective-permute-done | bytes 4194336 | tf_op jit(solution)/shard_map/ppermute | solution.py:12
  54.7 5.1 %fusion = f32[1024,768]{1,0:T(8,128)} fusion(bf16[1,1024,2048]{2,1,0:T(8,128)(2,1)S(1)} %collective-permute-done, bf16[1,2048,768]{2,1,0:T(8,128)(2,1)S(1)} %copy-done), kind=kOutput, calls=%fused_computation | convolution fusion | flops 3221225472 | bytes 10485760 | tf_op jit(solution)/shard_map/dot_general | solution.py:33
  59.8 43.8 %reduce-scatter.2.cloned.1.call-done = f32[256,768]{1,0:T(8,128)} async-done(((f32[1024,768]{1,0:T(8,128)}), f32[256,768]{1,0:T(8,128)}) %reduce-scatter.2.cloned.1.call-update) | async-done | bytes 786448 | tf_op jit(solution)/shard_map/reduce_scatter | solution.py:32
  104.8 1.8 maximum_bitcast_fusion.1
  106.6 8.4 %all-to-all-start = ((f32[32,1,8,512]{3,2,1,0:T(8,128)}), f32[32,1,8,512]{3,2,1,0:T(8,128)}, u32[]{:S(2)}, u32[]{:S(2)}) async-start(f32[32,1,8,512]{3,2,1,0:T(8,128)} %maximum_bitcast_fusion.1), calls=%async_computation.1 | async-start | bytes 1048576 | tf_op jit(solution)/shard_map/all_to_all | solution.py:16
  115.2 17.5 %all-to-all-done = f32[32,1,8,512]{3,2,1,0:T(8,128)} async-done(((f32[32,1,8,512]{3,2,1,0:T(8,128)}), f32[32,1,8,512]{3,2,1,0:T(8,128)}, u32[]{:S(2)}, u32[]{:S(2)}) %all-to-all-start) | async-done | bytes 524320 | tf_op jit(solution)/shard_map/all_to_all | solution.py:16
  132.7 2.3 fusion.22
  135.0 2.6 multiply_add_fusion
  137.8 2.5 copy.44
  140.3 5.0 %all-to-all-start.1 = ((f32[64,1,8,1024]{3,2,1,0:T(8,128)}), f32[64,1,8,1024]{3,2,1,0:T(8,128)}, u32[]{:S(2)}, u32[]{:S(2)}) async-start(f32[64,1,8,1024]{3,2,1,0:T(8,128)} %copy.44), calls=%async_computation.2 | async-start | bytes 4194304 | tf_op jit(solution)/shard_map/all_to_all | solution.py:16
  145.3 49.1 %all-to-all-done.1 = f32[64,1,8,1024]{3,2,1,0:T(8,128)} async-done(((f32[64,1,8,1024]{3,2,1,0:T(8,128)}), f32[64,1,8,1024]{3,2,1,0:T(8,128)}, u32[]{:S(2)}, u32[]{:S(2)}) %all-to-all-start.1) | async-done | bytes 2097184 | tf_op jit(solution)/shard_map/all_to_all | solution.py:16
  194.4 1.7 copy.87
  196.1 2.7 fusion.10
  198.8 2.7 fusion.12
  201.5 2.7 fusion.3
  204.1 2.7 fusion.4
  207.0 1.8 fusion.18
  208.8 1.6 fusion.16
  210.4 1.6 fusion.5
  212.0 1.6 fusion.6
  213.7 1.6 copy.52
  215.4 6.1 %all-to-all-start.2 = ((f32[32,2,8,512]{3,2,1,0:T(8,128)}), f32[32,2,8,512]{3,2,1,0:T(8,128)}, u32[]{:S(2)}, u32[]{:S(2)}) async-start(f32[32,2,8,512]{3,2,1,0:T(8,128)} %copy.52), calls=%async_computation.3 | async-start | bytes 2097152 | tf_op jit(solution)/shard_map/all_to_all | solution.py:16
  222.8 25.2 %all-to-all-done.2 = f32[32,2,8,512]{3,2,1,0:T(8,128)} async-done(((f32[32,2,8,512]{3,2,1,0:T(8,128)}), f32[32,2,8,512]{3,2,1,0:T(8,128)}, u32[]{:S(2)}, u32[]{:S(2)}) %all-to-all-start.2) | async-done | bytes 1048608 | tf_op jit(solution)/shard_map/all_to_all | solution.py:16
  250.8 17.1 %all_to_all.42 = f32[32,1,8,256]{3,2,1,0:T(8,128)S(1)} all-to-all(f32[32,1,8,256]{3,2,1,0:T(8,128)S(1)} %copy.57), channel_id=1, replica_groups=mesh['section'=8,'seq'=8,'chan'=4] {'seq','chan'}, dimensions={0} | all-to-all | bytes 524288 | tf_op jit(solution)/shard_map/all_to_all | solution.py:16
  (22 shorter events, 6.6 us)
Async XLA Ops:
  6.5 48.1 %copy-start = (bf16[1,2048,768]{2,1,0:T(8,128)(2,1)S(1)}, bf16[1,2048,768]{2,1,0:T(8,128)(2,1)}, u32[]{:S(2)}) copy-start(bf16[1,2048,768]{2,1,0:T(8,128)(2,1)} %param.5) | copy-start | bytes 9437188
  6.5 97.1 %reduce-scatter.2.cloned.1.call-start = ((), (), s32[]{:S(2)}) async-start(), calls=%async_computation.5 | async-start | bytes 3932160 | tf_op jit(solution)/shard_map/reduce_scatter | solution.py:32
  6.5 48.1 %collective-permute-start = (bf16[1,1024,2048]{2,1,0:T(8,128)(2,1)}, bf16[1,1024,2048]{2,1,0:T(8,128)(2,1)S(1)}, u32[]{:S(2)}, u32[]{:S(2)}) collective-permute-start(bf16[1,1024,2048]{2,1,0:T(8,128)(2,1)} %param.4), channel_id=1, source_target_pairs={{0,32},{32,64},{64,96},{96,128},{128,160},{160,192},{192,224},{224... | collective-permute-start | bytes 12582920 | tf_op jit(solution)/shard_map/ppermute | solution.py:12
  106.6 26.1 %all-to-all-start = ((f32[32,1,8,512]{3,2,1,0:T(8,128)}), f32[32,1,8,512]{3,2,1,0:T(8,128)}, u32[]{:S(2)}, u32[]{:S(2)}) async-start(f32[32,1,8,512]{3,2,1,0:T(8,128)} %maximum_bitcast_fusion.1), calls=%async_computation.1 | async-start | bytes 1048576 | tf_op jit(solution)/shard_map/all_to_all | solution.py:16
  140.3 54.1 %all-to-all-start.1 = ((f32[64,1,8,1024]{3,2,1,0:T(8,128)}), f32[64,1,8,1024]{3,2,1,0:T(8,128)}, u32[]{:S(2)}, u32[]{:S(2)}) async-start(f32[64,1,8,1024]{3,2,1,0:T(8,128)} %copy.44), calls=%async_computation.2 | async-start | bytes 4194304 | tf_op jit(solution)/shard_map/all_to_all | solution.py:16
  215.4 32.7 %all-to-all-start.2 = ((f32[32,2,8,512]{3,2,1,0:T(8,128)}), f32[32,2,8,512]{3,2,1,0:T(8,128)}, u32[]{:S(2)}, u32[]{:S(2)}) async-start(f32[32,2,8,512]{3,2,1,0:T(8,128)} %copy.52), calls=%async_computation.3 | async-start | bytes 2097152 | tf_op jit(solution)/shard_map/all_to_all | solution.py:16
  248.0 19.8 %copy-start.1 = (f32[1,256]{1,0:T(1,128)S(1)}, f32[1,256]{1,0:T(1,128)}, u32[]{:S(2)}) copy-start(f32[1,256]{1,0:T(1,128)} %param.7) | copy-start | bytes 3076
Sparse Core Ops, SparseCore 0:
  59.9 43.6 reduce-scatter.1
where the time goes:
time: 276 us; the launch traced here: 275 us
  waiting for transfers between devices  184 us (67%)
  matrix products  28.3 us (10%)
  starting transfers between devices  19.5 us (7%)
  blocking collectives  17.1 us (6%)
  between operations  13.6 us (5%)
  local copies, waits for them, and re-layouts  7.43 us (3%)
  other arithmetic  5.71 us (2%)
    all_to_all x3, waiting for transfers between devices, transpose_blocks(): lax.all_to_all(data, ('seq', 'chan'), split_axis=0, concat_axis=1, tiled=...  91.8 us
    ppermute x1, waiting for transfers between devices, from_behind(): return lax.ppermute(value, axis, pairs)  48.1 us
    reduce_scatter x1, waiting for transfers between devices, body(): lax.psum_scatter(jnp.dot(picked, in_weight[0], preferred_element_type=jnp...  43.8 us
    dot_general x12, matrix products, mix(): return jnp.einsum(form, table, data, precision=lax.Precision.HIGHEST)  23.3 us
    all_to_all x3, starting transfers between devices, transpose_blocks(): lax.all_to_all(data, ('seq', 'chan'), split_axis=0, concat_axis=1, tiled=...  19.5 us
    all_to_all x1, blocking collectives, transpose_blocks(): lax.all_to_all(data, ('seq', 'chan'), split_axis=0, concat_axis=1, tiled=...  17.1 us
  transfers between devices with their start and end apart: 5, of which 5 were waited for; matrix products, arithmetic and copies ran while one was open for 1% of the time, Pallas kernels for 0%

commit v1 on v0

v1 whole, which is shorter than its diff:
```python
import jax
import jax.numpy as jnp
from jax import lax
from jax.sharding import PartitionSpec as P


def from_behind(value, axis, steps):
    count = lax.axis_size(axis)
    pairs = [(source, (source + steps) % count) for source in range(count)]
    return lax.ppermute(value, axis, pairs)


def body(layer_rows, in_weight, long_filter, skip_gain):
    n_chan = lax.axis_size("chan")
    n_seq = lax.axis_size("seq")
    n_pos = n_chan * n_seq
    width = long_filter.shape[2]
    block_rows = long_filter.shape[1]
    seq_rows = layer_rows.shape[1]
    seq_len = block_rows * n_pos
    fft_length = 2 * seq_len
    chan_width = width // n_chan
    own = chan_width // n_seq
    q_index = lax.axis_index("seq")
    c_index = lax.axis_index("chan")

    taps = long_filter[0].reshape(block_rows, n_chan, n_seq, own)
    taps = taps.transpose(2, 1, 3, 0).reshape(n_pos, own, block_rows)
    taps = lax.all_to_all(taps, ("seq", "chan"), 0, 0, tiled=True)
    taps = taps.reshape(n_pos, own, block_rows).transpose(1, 0, 2).reshape(own, seq_len)
    taps_freq = jnp.fft.rfft(taps, n=fft_length, axis=-1)

    weight = in_weight[0].reshape(-1, 3, n_chan, chan_width)
    weight = weight.transpose(0, 2, 1, 3).reshape(-1, 3 * width)

    source = from_behind(layer_rows, "section", 1)[0]
    partial = jnp.einsum("fn,rf->nr", weight, source, preferred_element_type=jnp.float32)
    summed = lax.psum_scatter(partial, "chan", scatter_dimension=0, tiled=True)
    mixed = summed.astype(jnp.bfloat16).reshape(3, n_seq, own, seq_rows)
    mixed = mixed.transpose(1, 0, 2, 3)
    mixed = lax.all_to_all(mixed, "seq", 0, 0, tiled=True)
    mixed = mixed.reshape(n_seq, 3, own, seq_rows).transpose(1, 2, 0, 3).reshape(3, own, seq_len)
    queries = mixed[0].astype(jnp.float32)
    signal = mixed[1].astype(jnp.float32) * mixed[2].astype(jnp.float32)

    spectrum = jnp.fft.rfft(signal, n=fft_length, axis=-1) * taps_freq
    conv = jnp.fft.irfft(spectrum, n=fft_length, axis=-1)[:, :seq_len]
    gain = lax.dynamic_slice_in_dim(skip_gain[0], c_index * chan_width + q_index * own, own)
    gated = (queries * (conv + gain[:, None] * signal)).astype(jnp.bfloat16)

    gated = gated.reshape(own, n_pos, block_rows).transpose(1, 0, 2)
    gated = lax.all_to_all(gated, ("seq", "chan"), 0, 0, tiled=True)
    gated = gated.reshape(n_seq, n_chan, own, block_rows).transpose(3, 1, 0, 2)
    return gated.reshape(block_rows, width)[None]


def solution(mesh):
    in_specs = (
        P("section", "seq", "chan"),
        P("section", "chan", None),
        P("section", ("seq", "chan"), None),
        P("section", None),
    )
    out_specs = P("section", ("seq", "chan"), None)
    return jax.shard_map(body, mesh=mesh, in_specs=in_specs, out_specs=out_specs, check_vma=False)
```

time: 276 us -> 183 us (0.66)
  waiting for transfers between devices: 184 us -> 89.2 us
  local copies, waits for them, and re-layouts: 7.43 us -> 20.7 us
  matrix products: 28.3 us -> 24 us
  blocking collectives: 17.1 us -> 13.9 us
    all_to_all x3 -> x2, waiting for transfers between devices: 91.8 us -> 12.7 us  [the longest x1 12.7 us: body(): mixed = lax.all_to_all(mixed, 'seq', 0, 0, tiled=True)]
    dot_general x13 -> x1, matrix products: 28.3 us -> 7.3 us  [body(): jnp.einsum('fn,rf->nr', weight, source, preferred_element_type=jnp.float32)]
    another operation x0 -> x17, matrix products: none -> 16.7 us  [the longest x6 7.35 us: body(): conv = jnp.fft.irfft(spectrum, n=fft_length, axis=-1)[:, :seq_len]]
    unnamed x4 -> x18, local copies, waits for them, and re-layouts: 0.01 us -> 16.5 us
    reduce_scatter x1, waiting for transfers between devices: 43.8 us -> 31.9 us  [body(): summed = lax.psum_scatter(partial, 'chan', scatter_dimension=0, tiled=True)]
    ppermute x1, waiting for transfers between devices: 48.1 us -> 44.7 us  [from_behind(): return lax.ppermute(value, axis, pairs)]
    all_to_all x1, blocking collectives: 17.1 us -> 13.9 us  [body(): gated = lax.all_to_all(gated, ('seq', 'chan'), 0, 0, tiled=True)]
    all_to_all x3 -> x2, starting transfers between devices: 19.5 us -> 17.6 us  [the longest x1 11.3 us: body(): taps = lax.all_to_all(taps, ('seq', 'chan'), 0, 0, tiled=True)]
  transfers between devices with their start and end apart: 5 -> 4, of which waited for: 5 -> 3; matrix products, arithmetic and copies ran while one was open for 1% -> 5% of each run, Pallas kernels for 0% -> 0%
where the time goes in v1:
time: 183 us
  waiting for transfers between devices  89.2 us (49%)
  matrix products  24 us (13%)
  local copies, waits for them, and re-layouts  20.7 us (11%)
  starting transfers between devices  17.6 us (10%)
  blocking collectives  13.9 us (8%)
  between operations  13.8 us (8%)
  other arithmetic  3.51 us (2%)
    ppermute x1, waiting for transfers between devices, from_behind(): return lax.ppermute(value, axis, pairs)  44.7 us
    reduce_scatter x1, waiting for transfers between devices, body(): summed = lax.psum_scatter(partial, 'chan', scatter_dimension=0, tiled=True)  31.9 us
    unnamed x18, local copies, waits for them, and re-layouts  16.5 us
    all_to_all x1, blocking collectives, body(): gated = lax.all_to_all(gated, ('seq', 'chan'), 0, 0, tiled=True)  13.9 us
    all_to_all x1, waiting for transfers between devices, body(): mixed = lax.all_to_all(mixed, 'seq', 0, 0, tiled=True)  12.7 us
    all_to_all x1, starting transfers between devices, body(): taps = lax.all_to_all(taps, ('seq', 'chan'), 0, 0, tiled=True)  11.3 us
    another operation x6, matrix products, body(): conv = jnp.fft.irfft(spectrum, n=fft_length, axis=-1)[:, :seq_len]  7.35 us
    dot_general x1, matrix products, body(): jnp.einsum('fn,rf->nr', weight, source, preferred_element_type=jnp.float32)  7.3 us
  transfers between devices with their start and end apart: 4, of which 3 were waited for; matrix products, arithmetic and copies ran while one was open for 5% of the time, Pallas kernels for 0%

profile of v1, /device:TPU:8, one launch (start us, length us, event | category | flops | bytes accessed | tf_op | source)
XLA Modules:
  0.0 182.6 jit_solution(5457766153112522161)
XLA Ops:
  6.5 3.2 %copy.41 = bf16[1,2048,768]{1,2,0:T(8,128)(2,1)S(1)} copy(bf16[1,2048,768]{2,1,0:T(8,128)(2,1)} %param.6) | data formatting | bytes 6291456 | tf_op args[1]
  10.1 44.7 %collective-permute-done = bf16[1,1024,2048]{2,1,0:T(8,128)(2,1)} collective-permute-done((bf16[1,1024,2048]{2,1,0:T(8,128)(2,1)}, bf16[1,1024,2048]{2,1,0:T(8,128)(2,1)}, u32[]{:S(2)}, u32[]{:S(2)}) %collective-permute-start) | collective-permute-done | bytes 4194336 | tf_op jit(solution)/shard_map/ppermute | solution.py:10
  54.8 7.3 %fusion = f32[768,1024]{1,0:T(8,128)} fusion(bf16[2048,768]{0,1:T(8,128)(2,1)S(1)} %bitcast.169, bf16[1,1024,2048]{2,1,0:T(8,128)(2,1)} %collective-permute-done), kind=kOutput, calls=%fused_computation | convolution fusion | flops 3221225472 | bytes 10485760 | tf_op jit(solution)/shard_map/fn,rf->nr/dot_general | solution.py:37
  62.1 0.9 copy-done.2
  63.9 11.3 %all-to-all-start.1 = ((f32[32,8,256]{2,1,0:T(8,128)}), f32[32,8,256]{2,1,0:T(8,128)S(1)}, u32[]{:S(2)}, u32[]{:S(2)}) async-start(f32[32,8,256]{2,1,0:T(8,128)} %bitcast.20), calls=%async_computation.2 | async-start | bytes 524288 | tf_op jit(solution)/shard_map/all_to_all | solution.py:29
  76.6 31.9 %reduce-scatter.3.cloned.1.call-done = f32[192,1024]{1,0:T(8,128)} async-done(((f32[768,1024]{1,0:T(8,128)}), f32[192,1024]{1,0:T(8,128)}) %reduce-scatter.3.cloned.1.call-update) | async-done | bytes 786448 | tf_op jit(solution)/shard_map/reduce_scatter | solution.py:38
  108.5 1.2 convert_element_type.22
  110.5 6.3 %all-to-all-start = ((bf16[8,3,8,1024]{3,2,1,0:T(8,128)(2,1)}), bf16[8,3,8,1024]{3,2,1,0:T(8,128)(2,1)S(1)}, u32[]{:S(2)}, u32[]{:S(2)}) async-start(bf16[8,3,8,1024]{3,2,1,0:T(8,128)(2,1)} %bitcast.167), calls=%async_computation.1 | async-start | bytes 786432 | tf_op jit(solution)/shard_map/all_to_all | solution.py:41
  118.0 0.9 fusion.3
  118.9 12.7 %all-to-all-done = bf16[8,3,8,1024]{3,2,1,0:T(8,128)(2,1)S(1)} async-done(((bf16[8,3,8,1024]{3,2,1,0:T(8,128)(2,1)}), bf16[8,3,8,1024]{3,2,1,0:T(8,128)(2,1)S(1)}, u32[]{:S(2)}, u32[]{:S(2)}) %all-to-all-start) | async-done | bytes 393248 | tf_op jit(solution)/shard_map/all_to_all | solution.py:41
  131.7 0.9 convolution_bitcast_fusion.4
  132.5 1.1 multiply_add_fusion.1
  138.8 1.1 copy.136
  140.7 1.1 copy.134
  142.3 1.0 multiply_subtract_fusion.3
  143.5 4.5 %reverse.3 = f32[8,8192]{1,0:T(8,128)S(1)} reverse(f32[8,8192]{1,0:T(8,128)S(1)} %bitcast.187), dimensions={1} | reverse | bytes 524288
  148.3 4.5 %reverse.2 = f32[8,8192]{1,0:T(8,128)S(1)} reverse(f32[8,8192]{1,0:T(8,128)S(1)} %bitcast.188), dimensions={1} | reverse | bytes 524288
  153.1 1.3 fusion.15
  154.4 1.2 fusion.9
  155.6 1.2 fusion.8
  156.8 1.3 fusion.26
  158.1 1.2 fusion.7
  159.3 1.2 fusion.6
  161.2 13.9 %all_to_all.15 = bf16[32,8,256]{2,1,0:T(8,128)(2,1)S(1)} all-to-all(bf16[32,8,256]{2,1,0:T(8,128)(2,1)S(1)} %bitcast.192), channel_id=1, replica_groups=mesh['section'=8,'seq'=8,'chan'=4] {'seq','chan'}, dimensions={0} | all-to-all | bytes 262144 | tf_op jit(solution)/shard_map/all_to_all | solution.py:52
  (48 shorter events, 13.1 us)
Async XLA Ops:
  6.5 110.2 %copy-start = (f32[1,256]{1,0:T(1,128)S(1)}, f32[1,256]{1,0:T(1,128)}, u32[]{:S(2)}) copy-start(f32[1,256]{1,0:T(1,128)} %param.8) | copy-start | bytes 3076
  6.5 102.0 %reduce-scatter.3.cloned.1.call-start = ((), (), s32[]{:S(2)}) async-start(), calls=%async_computation.4 | async-start | bytes 3932160 | tf_op jit(solution)/shard_map/reduce_scatter | solution.py:38
  6.5 48.2 %collective-permute-start = (bf16[1,1024,2048]{2,1,0:T(8,128)(2,1)}, bf16[1,1024,2048]{2,1,0:T(8,128)(2,1)}, u32[]{:S(2)}, u32[]{:S(2)}) collective-permute-start(bf16[1,1024,2048]{2,1,0:T(8,128)(2,1)} %param.5), channel_id=1, source_target_pairs={{0,32},{32,64},{64,96},{96,128},{128,160},{160,192},{192,224},{224... | collective-permute-start | bytes 12582920 | tf_op jit(solution)/shard_map/ppermute | solution.py:10
  62.1 0.9 copy-start.2
  63.9 46.6 %all-to-all-start.1 = ((f32[32,8,256]{2,1,0:T(8,128)}), f32[32,8,256]{2,1,0:T(8,128)S(1)}, u32[]{:S(2)}, u32[]{:S(2)}) async-start(f32[32,8,256]{2,1,0:T(8,128)} %bitcast.20), calls=%async_computation.2 | async-start | bytes 524288 | tf_op jit(solution)/shard_map/all_to_all | solution.py:29
  110.5 21.1 %all-to-all-start = ((bf16[8,3,8,1024]{3,2,1,0:T(8,128)(2,1)}), bf16[8,3,8,1024]{3,2,1,0:T(8,128)(2,1)S(1)}, u32[]{:S(2)}, u32[]{:S(2)}) async-start(bf16[8,3,8,1024]{3,2,1,0:T(8,128)(2,1)} %bitcast.167), calls=%async_computation.1 | async-start | bytes 786432 | tf_op jit(solution)/shard_map/all_to_all | solution.py:41
  139.9 2.3 %copy-start.1 = (f32[1,8,128,128]{3,1,2,0:T(8,128)S(1)}, f32[1,8,128,128]{3,1,2,0:T(8,128)}, u32[]{:S(2)}) copy-start(f32[1,8,128,128]{3,1,2,0:T(8,128)} %copy.136) | copy-start | bytes 1572868
Sparse Core Ops, SparseCore 0:
  62.2 46.2 reduce-scatter.2

commit v2 on v1

--- a/solution.py
+++ b/solution.py
@@ -2,6 +2,9 @@
 import jax.numpy as jnp
 from jax import lax
 from jax.sharding import PartitionSpec as P
+
+
+CHUNKS = 4
 
 
 def from_behind(value, axis, steps):
@@ -33,10 +36,15 @@
     weight = in_weight[0].reshape(-1, 3, n_chan, chan_width)
     weight = weight.transpose(0, 2, 1, 3).reshape(-1, 3 * width)
 
-    source = from_behind(layer_rows, "section", 1)[0]
-    partial = jnp.einsum("fn,rf->nr", weight, source, preferred_element_type=jnp.float32)
-    summed = lax.psum_scatter(partial, "chan", scatter_dimension=0, tiled=True)
-    mixed = summed.astype(jnp.bfloat16).reshape(3, n_seq, own, seq_rows)
+    pieces = []
+    chunk_rows = seq_rows // CHUNKS
+    for chunk in range(CHUNKS):
+        rows = layer_rows[:, chunk * chunk_rows : (chunk + 1) * chunk_rows]
+        source = from_behind(rows, "section", 1)[0]
+        partial = jnp.einsum("fn,rf->nr", weight, source, preferred_element_type=jnp.float32)
+        summed = lax.psum_scatter(partial, "chan", scatter_dimension=0, tiled=True)
+        pieces.append(summed.astype(jnp.bfloat16))
+    mixed = jnp.concatenate(pieces, axis=1).reshape(3, n_seq, own, seq_rows)
     mixed = mixed.transpose(1, 0, 2, 3)
     mixed = lax.all_to_all(mixed, "seq", 0, 0, tiled=True)
     mixed = mixed.reshape(n_seq, 3, own, seq_rows).transpose(1, 2, 0, 3).reshape(3, own, seq_len)

time: 183 us -> 212 us (1.16)
  waiting for transfers between devices: 89.2 us -> 108 us
  matrix products: 24 us -> 27.6 us
  local copies, waits for them, and re-layouts: 20.7 us -> 24.1 us
  other arithmetic: 3.51 us -> 6.11 us
    reduce_scatter x1 -> x4, waiting for transfers between devices: 31.9 us -> 42.8 us  [body(): summed = lax.psum_scatter(partial, 'chan', scatter_dimension=0, tiled=True)]
    ppermute x1 -> x4, waiting for transfers between devices: 44.7 us -> 54.4 us  [from_behind(): return lax.ppermute(value, axis, pairs)]
    slice x0 -> x1, local copies, waits for them, and re-layouts: none -> 4.44 us  [body(): rows = layer_rows[:, chunk * chunk_rows:(chunk + 1) * chunk_rows]]
    dot_general x1 -> x4, matrix products: 7.3 us -> 10.9 us  [body(): jnp.einsum('fn,rf->nr', weight, source, preferred_element_type=jnp.float32)]
    convert_element_type x1 -> x4, other arithmetic: 1.18 us -> 3.75 us  [body(): pieces.append(summed.astype(jnp.bfloat16))]
    all_to_all x1, waiting for transfers between devices: 12.7 us -> 10.5 us  [body(): mixed = lax.all_to_all(mixed, 'seq', 0, 0, tiled=True)]
    unnamed x18 -> x22, local copies, waits for them, and re-layouts: 16.5 us -> 15.6 us
  transfers between devices with their start and end apart: 4 -> 10, of which waited for: 3 -> 7; matrix products, arithmetic and copies ran while one was open for 5% -> 10% of each run, Pallas kernels for 0% -> 0%
where the time goes in v2:
time: 212 us; the launch traced here: 211 us
  waiting for transfers between devices  108 us (51%)
  matrix products  27.6 us (13%)
  local copies, waits for them, and re-layouts  24.1 us (11%)
  starting transfers between devices  18.4 us (9%)
  blocking collectives  13.7 us (6%)
  between operations  13.6 us (6%)
  other arithmetic  6.11 us (3%)
    ppermute x4, waiting for transfers between devices, from_behind(): return lax.ppermute(value, axis, pairs)  54.4 us
    reduce_scatter x4, waiting for transfers between devices, body(): summed = lax.psum_scatter(partial, 'chan', scatter_dimension=0, tiled=True)  42.8 us
    unnamed x22, local copies, waits for them, and re-layouts  15.6 us
    all_to_all x1, blocking collectives, body(): gated = lax.all_to_all(gated, ('seq', 'chan'), 0, 0, tiled=True)  13.7 us
    all_to_all x1, starting transfers between devices, body(): taps = lax.all_to_all(taps, ('seq', 'chan'), 0, 0, tiled=True)  11.3 us
    dot_general x4, matrix products, body(): jnp.einsum('fn,rf->nr', weight, source, preferred_element_type=jnp.float32)  10.9 us
    all_to_all x1, waiting for transfers between devices, body(): mixed = lax.all_to_all(mixed, 'seq', 0, 0, tiled=True)  10.5 us
    another operation x6, matrix products, body(): conv = jnp.fft.irfft(spectrum, n=fft_length, axis=-1)[:, :seq_len]  7.35 us
  transfers between devices with their start and end apart: 10, of which 7 were waited for; matrix products, arithmetic and copies ran while one was open for 10% of the time, Pallas kernels for 0%

profile of v2, /device:TPU:8, one launch (start us, length us, event | category | flops | bytes accessed | tf_op | source)
XLA Modules:
  0.0 211.2 jit_solution(15469333511791657331)
XLA Ops:
  6.5 4.4 %fusion.161 = (bf16[1,256,2048]{2,1,0:T(8,128)(2,1)}, bf16[1,256,2048]{2,1,0:T(8,128)(2,1)}, bf16[1,256,2048]{2,1,0:T(8,128)(2,1)}, bf16[1,256,2048]{2,1,0:T(8,128)(2,1)}) fusion(bf16[1,1024,2048]{2,1,0:T(8,128)(2,1)} %param.5), kind=kLoop, calls=%fused_computation.185 | loop fusion | bytes 8388608 | tf_op jit(solution)/shard_map/slice | solution.py:42
  11.0 3.2 %copy.41 = bf16[1,2048,768]{1,2,0:T(8,128)(2,1)S(1)} copy(bf16[1,2048,768]{2,1,0:T(8,128)(2,1)} %param.6) | data formatting | bytes 6291456 | tf_op args[1]
  14.4 11.1 %collective-permute-done = bf16[1,256,2048]{2,1,0:T(8,128)(2,1)} collective-permute-done((bf16[1,256,2048]{2,1,0:T(8,128)(2,1)}, bf16[1,256,2048]{2,1,0:T(8,128)(2,1)}, u32[]{:S(2)}, u32[]{:S(2)}) %collective-permute-start) | collective-permute-done | bytes 1048608 | tf_op jit(solution)/shard_map/ppermute | solution.py:13
  25.5 3.2 %fusion.18 = f32[768,256]{1,0:T(8,128)} fusion(bf16[2048,768]{0,1:T(8,128)(2,1)S(1)} %bitcast.181, bf16[1,256,2048]{2,1,0:T(8,128)(2,1)} %collective-permute-done), kind=kOutput, calls=%fused_computation.31 | convolution fusion | flops 805306368 | bytes 4980736 | tf_op jit(solution)/shard_map/fn,rf->nr/dot_general | solution.py:44
  28.8 14.4 %collective-permute-done.1 = bf16[1,256,2048]{2,1,0:T(8,128)(2,1)S(1)} collective-permute-done((bf16[1,256,2048]{2,1,0:T(8,128)(2,1)}, bf16[1,256,2048]{2,1,0:T(8,128)(2,1)S(1)}, u32[]{:S(2)}, u32[]{:S(2)}) %collective-permute-start.1) | collective-permute-done | bytes 1048608 | tf_op jit(solution)/shard_map/ppermute | solution.py:13
  43.2 3.9 %fusion.16 = f32[768,256]{1,0:T(8,128)} fusion(bf16[2048,768]{0,1:T(8,128)(2,1)} %bitcast.182, bf16[1,256,2048]{2,1,0:T(8,128)(2,1)S(1)} %collective-permute-done.1), kind=kOutput, calls=%fused_computation.29 | convolution fusion | flops 805306368 | bytes 4980736 | tf_op jit(solution)/shard_map/fn,rf->nr/dot_general | solution.py:44
  47.2 14.4 %collective-permute-done.2 = bf16[1,256,2048]{2,1,0:T(8,128)(2,1)S(1)} collective-permute-done((bf16[1,256,2048]{2,1,0:T(8,128)(2,1)}, bf16[1,256,2048]{2,1,0:T(8,128)(2,1)S(1)}, u32[]{:S(2)}, u32[]{:S(2)}) %collective-permute-start.2) | collective-permute-done | bytes 1048608 | tf_op jit(solution)/shard_map/ppermute | solution.py:13
  61.6 2.0 fusion.14
  63.7 14.4 %collective-permute-done.3 = bf16[1,256,2048]{2,1,0:T(8,128)(2,1)S(1)} collective-permute-done((bf16[1,256,2048]{2,1,0:T(8,128)(2,1)}, bf16[1,256,2048]{2,1,0:T(8,128)(2,1)S(1)}, u32[]{:S(2)}, u32[]{:S(2)}) %collective-permute-start.3) | collective-permute-done | bytes 1048608 | tf_op jit(solution)/shard_map/ppermute | solution.py:13
  78.1 2.0 fusion.12
  81.0 11.3 %all-to-all-start.1 = ((f32[32,8,256]{2,1,0:T(8,128)}), f32[32,8,256]{2,1,0:T(8,128)S(1)}, u32[]{:S(2)}, u32[]{:S(2)}) async-start(f32[32,8,256]{2,1,0:T(8,128)} %bitcast.23), calls=%async_computation.5 | async-start | bytes 524288 | tf_op jit(solution)/shard_map/all_to_all | solution.py:32
  95.6 16.9 %reduce-scatter.13.cloned.1.call-done = f32[192,256]{1,0:T(8,128)} async-done(((f32[768,256]{1,0:T(8,128)}), f32[192,256]{1,0:T(8,128)}) %reduce-scatter.13.cloned.1.call-update) | async-done | bytes 196624 | tf_op jit(solution)/shard_map/reduce_scatter | solution.py:45
  113.5 25.9 %reduce-scatter.15.cloned.1.call-done = f32[192,256]{1,0:T(8,128)} async-done(((f32[768,256]{1,0:T(8,128)}), f32[192,256]{1,0:T(8,128)}) %reduce-scatter.15.cloned.1.call-update) | async-done | bytes 196624 | tf_op jit(solution)/shard_map/reduce_scatter | solution.py:45
  141.1 7.0 %all-to-all-start = ((bf16[8,3,8,1024]{3,2,1,0:T(8,128)(2,1)}), bf16[8,3,8,1024]{3,2,1,0:T(8,128)(2,1)S(1)}, u32[]{:S(2)}, u32[]{:S(2)}) async-start(bf16[8,3,8,1024]{3,2,1,0:T(8,128)(2,1)} %bitcast.179), calls=%async_computation.4 | async-start | bytes 786432 | tf_op jit(solution)/shard_map/all_to_all | solution.py:49
  150.2 10.5 %all-to-all-done = bf16[8,3,8,1024]{3,2,1,0:T(8,128)(2,1)S(1)} async-done(((bf16[8,3,8,1024]{3,2,1,0:T(8,128)(2,1)}), bf16[8,3,8,1024]{3,2,1,0:T(8,128)(2,1)S(1)}, u32[]{:S(2)}, u32[]{:S(2)}) %all-to-all-start) | async-done | bytes 393248 | tf_op jit(solution)/shard_map/all_to_all | solution.py:49
  172.5 4.5 %reverse.3 = f32[8,8192]{1,0:T(8,128)S(1)} reverse(f32[8,8192]{1,0:T(8,128)S(1)} %bitcast.202), dimensions={1} | reverse | bytes 524288
  177.4 4.5 %reverse.2 = f32[8,8192]{1,0:T(8,128)S(1)} reverse(f32[8,8192]{1,0:T(8,128)S(1)} %bitcast.203), dimensions={1} | reverse | bytes 524288
  182.2 1.3 fusion.21
  183.4 1.2 fusion.7
  184.7 1.2 fusion.6
  185.9 1.3 fusion.32
  187.1 1.2 fusion.5
  188.4 1.2 fusion.4
  190.2 13.7 %all_to_all.15 = bf16[32,8,256]{2,1,0:T(8,128)(2,1)S(1)} all-to-all(bf16[32,8,256]{2,1,0:T(8,128)(2,1)S(1)} %bitcast.207), channel_id=1, replica_groups=mesh['section'=8,'seq'=8,'chan'=4] {'seq','chan'}, dimensions={0} | all-to-all | bytes 262144 | tf_op jit(solution)/shard_map/all_to_all | solution.py:60
  (75 shorter events, 23.3 us)
Async XLA Ops:
  6.5 141.5 %copy-start = (f32[1,256]{1,0:T(1,128)S(1)}, f32[1,256]{1,0:T(1,128)}, u32[]{:S(2)}) copy-start(f32[1,256]{1,0:T(1,128)} %param.8) | copy-start | bytes 3076
  6.5 87.2 %reduce-scatter.9.cloned.1.call-start = ((), (), s32[]{:S(2)}) async-start(), calls=%async_computation.7 | async-start | bytes 983040 | tf_op jit(solution)/shard_map/reduce_scatter | solution.py:45
  11.0 14.5 %collective-permute-start = (bf16[1,256,2048]{2,1,0:T(8,128)(2,1)}, bf16[1,256,2048]{2,1,0:T(8,128)(2,1)}, u32[]{:S(2)}, u32[]{:S(2)}) collective-permute-start(bf16[1,256,2048]{2,1,0:T(8,128)(2,1)} %get-tuple-element.16), channel_id=1, source_target_pairs={{0,32},{32,64},{64,96},{96,128},{128,160},{160,192},{192,224},{224... | collective-permute-start | bytes 3145736 | tf_op jit(solution)/shard_map/ppermute | solution.py:13
  14.4 11.1 %copy-start.1 = (bf16[2048,4,3,64]{0,3,2,1:T(8,128)(2,1)}, bf16[2048,4,3,64]{0,3,2,1:T(8,128)(2,1)S(1)}, u32[]{:S(2)}) copy-start(bf16[2048,4,3,64]{0,3,2,1:T(8,128)(2,1)S(1)} %copy.42) | copy-start | bytes 9437188
  28.7 66.0 %reduce-scatter.11.cloned.1.call-start = ((), (), s32[]{:S(2)}) async-start(), calls=%async_computation.8 | async-start | bytes 983040 | tf_op jit(solution)/shard_map/reduce_scatter | solution.py:45
  28.8 32.8 %copy-start.2 = (bf16[2048,4,3,64]{0,3,2,1:T(8,128)(2,1)S(1)}, bf16[2048,4,3,64]{0,3,2,1:T(8,128)(2,1)}, u32[]{:S(2)}) copy-start(bf16[2048,4,3,64]{0,3,2,1:T(8,128)(2,1)} %copy-done.1) | copy-start | bytes 9437188
  28.8 14.4 %collective-permute-start.1 = (bf16[1,256,2048]{2,1,0:T(8,128)(2,1)}, bf16[1,256,2048]{2,1,0:T(8,128)(2,1)S(1)}, u32[]{:S(2)}, u32[]{:S(2)}) collective-permute-start(bf16[1,256,2048]{2,1,0:T(8,128)(2,1)} %get-tuple-element.17), channel_id=1, source_target_pairs={{0,32},{32,64},{64,96},{96,128},{128,160},{160,192},{192,224},{224... | collective-permute-start | bytes 3145736 | tf_op jit(solution)/shard_map/ppermute | solution.py:13
  47.1 65.4 %reduce-scatter.13.cloned.1.call-start = ((), (), s32[]{:S(2)}) async-start(), calls=%async_computation.9 | async-start | bytes 983040 | tf_op jit(solution)/shard_map/reduce_scatter | solution.py:45
  47.1 14.4 %collective-permute-start.2 = (bf16[1,256,2048]{2,1,0:T(8,128)(2,1)}, bf16[1,256,2048]{2,1,0:T(8,128)(2,1)S(1)}, u32[]{:S(2)}, u32[]{:S(2)}) collective-permute-start(bf16[1,256,2048]{2,1,0:T(8,128)(2,1)} %get-tuple-element.19), channel_id=1, source_target_pairs={{0,32},{32,64},{64,96},{96,128},{128,160},{160,192},{192,224},{224... | collective-permute-start | bytes 3145736 | tf_op jit(solution)/shard_map/ppermute | solution.py:13
  63.6 75.7 %reduce-scatter.15.cloned.1.call-start = ((), (), s32[]{:S(2)}) async-start(), calls=%async_computation.10 | async-start | bytes 983040 | tf_op jit(solution)/shard_map/reduce_scatter | solution.py:45
  63.6 16.5 %copy-start.4 = (f32[1,256,256]{2,1,0:T(8,128)S(1)}, f32[1,256,256]{2,1,0:T(8,128)}, u32[]{:S(2)}) copy-start(f32[1,256,256]{2,1,0:T(8,128)} %param.7) | copy-start | bytes 786436
  63.6 14.4 %collective-permute-start.3 = (bf16[1,256,2048]{2,1,0:T(8,128)(2,1)}, bf16[1,256,2048]{2,1,0:T(8,128)(2,1)S(1)}, u32[]{:S(2)}, u32[]{:S(2)}) collective-permute-start(bf16[1,256,2048]{2,1,0:T(8,128)(2,1)} %get-tuple-element.18), channel_id=1, source_target_pairs={{0,32},{32,64},{64,96},{96,128},{128,160},{160,192},{192,224},{224... | collective-permute-start | bytes 3145736 | tf_op jit(solution)/shard_map/ppermute | solution.py:13
  81.0 60.1 %all-to-all-start.1 = ((f32[32,8,256]{2,1,0:T(8,128)}), f32[32,8,256]{2,1,0:T(8,128)S(1)}, u32[]{:S(2)}, u32[]{:S(2)}) async-start(f32[32,8,256]{2,1,0:T(8,128)} %bitcast.23), calls=%async_computation.5 | async-start | bytes 524288 | tf_op jit(solution)/shard_map/all_to_all | solution.py:32
  141.1 19.5 %all-to-all-start = ((bf16[8,3,8,1024]{3,2,1,0:T(8,128)(2,1)}), bf16[8,3,8,1024]{3,2,1,0:T(8,128)(2,1)S(1)}, u32[]{:S(2)}, u32[]{:S(2)}) async-start(bf16[8,3,8,1024]{3,2,1,0:T(8,128)(2,1)} %bitcast.179), calls=%async_computation.4 | async-start | bytes 786432 | tf_op jit(solution)/shard_map/all_to_all | solution.py:49
  169.0 2.3 %copy-start.3 = (f32[1,8,128,128]{3,1,2,0:T(8,128)S(1)}, f32[1,8,128,128]{3,1,2,0:T(8,128)}, u32[]{:S(2)}) copy-start(f32[1,8,128,128]{3,1,2,0:T(8,128)} %copy.136) | copy-start | bytes 1572868
Sparse Core Ops, SparseCore 0:
  28.8 28.0 reduce-scatter.8
  59.4 24.9 reduce-scatter.10
  87.0 25.4 reduce-scatter.12
  114.9 24.3 reduce-scatter.14

commit v3 on v2

--- a/solution.py
+++ b/solution.py
@@ -1,10 +1,55 @@
+import math
+
+import numpy as np
 import jax
 import jax.numpy as jnp
 from jax import lax
 from jax.sharding import PartitionSpec as P
 
 
-CHUNKS = 4
+CHUNKS = 2
+HI = lax.Precision.HIGHEST
+
+
+def dft_tables(seq_len):
+    fft_length = 2 * seq_len
+    side = int(round(math.sqrt(fft_length)))
+    half = seq_len // side
+    k = np.arange(side)
+    m = np.arange(half)
+    outer = 2 * np.pi * np.outer(k, m) / side
+    fine = 2 * np.pi * (np.outer(k, k) % side) / side
+    twist = 2 * np.pi * (np.outer(k, k) % fft_length) / fft_length
+    f32 = lambda a: jnp.asarray(a, dtype=jnp.float32)
+    return dict(
+        side=side, half=half,
+        a_cos=f32(np.cos(outer)), a_sin=f32(np.sin(outer)),
+        c_cos=f32(np.cos(fine)), c_sin=f32(np.sin(fine)),
+        t_cos=f32(np.cos(twist)), t_sin=f32(np.sin(twist)),
+        i_cos=f32(np.cos(outer) / fft_length), i_sin=f32(np.sin(outer) / fft_length),
+    )
+
+
+def forward(x, t):
+    c = x.shape[0]
+    x = x.reshape(c, t["half"], t["side"])
+    y_re = jnp.einsum("km,cmr->ckr", t["a_cos"], x, precision=HI)
+    y_im = -jnp.einsum("km,cmr->ckr", t["a_sin"], x, precision=HI)
+    z_re = y_re * t["t_cos"] + y_im * t["t_sin"]
+    z_im = y_im * t["t_cos"] - y_re * t["t_sin"]
+    s_re = jnp.einsum("ckr,rj->ckj", z_re, t["c_cos"], precision=HI) + jnp.einsum("ckr,rj->ckj", z_im, t["c_sin"], precision=HI)
+    s_im = jnp.einsum("ckr,rj->ckj", z_im, t["c_cos"], precision=HI) - jnp.einsum("ckr,rj->ckj", z_re, t["c_sin"], precision=HI)
+    return s_re, s_im
+
+
+def inverse(p_re, p_im, t):
+    c = p_re.shape[0]
+    u_re = jnp.einsum("ckj,jr->ckr", p_re, t["c_cos"], precision=HI) - jnp.einsum("ckj,jr->ckr", p_im, t["c_sin"], precision=HI)
+    u_im = jnp.einsum("ckj,jr->ckr", p_im, t["c_cos"], precision=HI) + jnp.einsum("ckj,jr->ckr", p_re, t["c_sin"], precision=HI)
+    v_re = u_re * t["t_cos"] - u_im * t["t_sin"]
+    v_im = u_im * t["t_cos"] + u_re * t["t_sin"]
+    out = jnp.einsum("km,ckr->cmr", t["i_cos"], v_re, precision=HI) - jnp.einsum("km,ckr->cmr", t["i_sin"], v_im, precision=HI)
+    return out.reshape(c, -1)
 
 
 def from_behind(value, axis, steps):
@@ -21,17 +66,18 @@
     block_rows = long_filter.shape[1]
     seq_rows = layer_rows.shape[1]
     seq_len = block_rows * n_pos
-    fft_length = 2 * seq_len
     chan_width = width // n_chan
     own = chan_width // n_seq
     q_index = lax.axis_index("seq")
     c_index = lax.axis_index("chan")
 
+    tables = dft_tables(seq_len)
+
     taps = long_filter[0].reshape(block_rows, n_chan, n_seq, own)
     taps = taps.transpose(2, 1, 3, 0).reshape(n_pos, own, block_rows)
     taps = lax.all_to_all(taps, ("seq", "chan"), 0, 0, tiled=True)
     taps = taps.reshape(n_pos, own, block_rows).transpose(1, 0, 2).reshape(own, seq_len)
-    taps_freq = jnp.fft.rfft(taps, n=fft_length, axis=-1)
+    taps_re, taps_im = forward(taps, tables)
 
     weight = in_weight[0].reshape(-1, 3, n_chan, chan_width)
     weight = weight.transpose(0, 2, 1, 3).reshape(-1, 3 * width)
@@ -51,8 +97,10 @@
     queries = mixed[0].astype(jnp.float32)
     signal = mixed[1].astype(jnp.float32) * mixed[2].astype(jnp.float32)
 
-    spectrum = jnp.fft.rfft(signal, n=fft_length, axis=-1) * taps_freq
-    conv = jnp.fft.irfft(spectrum, n=fft_length, axis=-1)[:, :seq_len]
+    sig_re, sig_im = forward(signal, tables)
+    prod_re = sig_re * taps_re - sig_im * taps_im
+    prod_im = sig_re * taps_im + sig_im * taps_re
+    conv = inverse(prod_re, prod_im, tables)
     gain = lax.dynamic_slice_in_dim(skip_gain[0], c_index * chan_width + q_index * own, own)
     gated = (queries * (conv + gain[:, None] * signal)).astype(jnp.bfloat16)
 

time: 212 us -> 166 us (0.78)
  waiting for transfers between devices: 108 us -> 78.5 us
  local copies, waits for them, and re-layouts: 24.1 us -> 14.2 us
  other arithmetic: 6.11 us -> 2.93 us
  matrix products: 27.6 us -> 25 us
    reduce_scatter x4 -> x2, waiting for transfers between devices: 42.8 us -> 5.85 us  [body(): summed = lax.psum_scatter(partial, 'chan', scatter_dimension=0, tiled=True)]
    another operation x17 -> x0, matrix products: 16.7 us -> none  [the longest x6 7.35 us: body(): conv = jnp.fft.irfft(spectrum, n=fft_length, axis=-1)[:, :seq_len]]
    dot_general x0 -> x18, matrix products: none -> 15.4 us  [the longest x2 2.61 us: forward(): jnp.einsum('ckr,rj->ckj', z_im, t['c_sin'], precision=HI)]
    all_to_all x1, waiting for transfers between devices: 0.01 us -> 12.3 us  [body(): taps = lax.all_to_all(taps, ('seq', 'chan'), 0, 0, tiled=True)]
    unnamed x22 -> x30, local copies, waits for them, and re-layouts: 15.6 us -> 3.4 us
    ppermute x4 -> x2, waiting for transfers between devices: 54.4 us -> 47.8 us  [from_behind(): return lax.ppermute(value, axis, pairs)]
    convert_element_type x0 -> x2, local copies, waits for them, and re-layouts: none -> 2.84 us  [body(): queries = mixed[0].astype(jnp.float32)]
    dot_general x4 -> x2, matrix products: 10.9 us -> 9.64 us  [body(): jnp.einsum('fn,rf->nr', weight, source, preferred_element_type=jnp.float32)]
  transfers between devices with their start and end apart: 10 -> 6, of which waited for: 7 -> 5; matrix products, arithmetic and copies ran while one was open for 10% -> 8% of each run, Pallas kernels for 0% -> 0%
where the time goes in v3:
time: 166 us
  waiting for transfers between devices  78.5 us (47%)
  matrix products  25 us (15%)
  starting transfers between devices  17.3 us (10%)
  local copies, waits for them, and re-layouts  14.2 us (9%)
  blocking collectives  13.8 us (8%)
  between operations  13.8 us (8%)
  other arithmetic  2.93 us (2%)
    ppermute x2, waiting for transfers between devices, from_behind(): return lax.ppermute(value, axis, pairs)  47.8 us
    all_to_all x1, blocking collectives, body(): gated = lax.all_to_all(gated, ('seq', 'chan'), 0, 0, tiled=True)  13.8 us
    all_to_all x1, waiting for transfers between devices, body(): mixed = lax.all_to_all(mixed, 'seq', 0, 0, tiled=True)  12.5 us
    all_to_all x1, waiting for transfers between devices, body(): taps = lax.all_to_all(taps, ('seq', 'chan'), 0, 0, tiled=True)  12.3 us
    all_to_all x1, starting transfers between devices, body(): taps = lax.all_to_all(taps, ('seq', 'chan'), 0, 0, tiled=True)  11.3 us
    dot_general x2, matrix products, body(): jnp.einsum('fn,rf->nr', weight, source, preferred_element_type=jnp.float32)  9.64 us
    all_to_all x1, starting transfers between devices, body(): mixed = lax.all_to_all(mixed, 'seq', 0, 0, tiled=True)  5.89 us
    reduce_scatter x2, waiting for transfers between devices, body(): summed = lax.psum_scatter(partial, 'chan', scatter_dimension=0, tiled=True)  5.85 us
  transfers between devices with their start and end apart: 6, of which 5 were waited for; matrix products, arithmetic and copies ran while one was open for 8% of the time, Pallas kernels for 0%

profile of v3, /device:TPU:8, one launch (start us, length us, event | category | flops | bytes accessed | tf_op | source)
XLA Modules:
  0.0 165.5 jit_solution(11909272940091347678)
XLA Ops:
  6.5 4.8 %fusion.26 = (bf16[1,512,2048]{2,1,0:T(8,128)(2,1)}, bf16[1,512,2048]{2,1,0:T(8,128)(2,1)}) fusion(bf16[1,1024,2048]{2,1,0:T(8,128)(2,1)} %param.12), kind=kLoop, calls=%fused_computation.48 | loop fusion | bytes 8388608 | tf_op jit(solution)/shard_map/slice | solution.py:88
  11.4 3.2 %copy.88 = bf16[1,2048,768]{1,2,0:T(8,128)(2,1)S(1)} copy(bf16[1,2048,768]{2,1,0:T(8,128)(2,1)} %param.13) | data formatting | bytes 6291456 | tf_op args[1]
  14.8 22.3 %collective-permute-done.1 = bf16[1,512,2048]{2,1,0:T(8,128)(2,1)} collective-permute-done((bf16[1,512,2048]{2,1,0:T(8,128)(2,1)}, bf16[1,512,2048]{2,1,0:T(8,128)(2,1)}, u32[]{:S(2)}, u32[]{:S(2)}) %collective-permute-start.1) | collective-permute-done | bytes 2097184 | tf_op jit(solution)/shard_map/ppermute | solution.py:58
  37.1 4.7 %fusion = f32[768,512]{1,0:T(8,128)} fusion(bf16[2048,768]{0,1:T(8,128)(2,1)S(1)} %bitcast.85, bf16[1,512,2048]{2,1,0:T(8,128)(2,1)} %collective-permute-done.1), kind=kOutput, calls=%fused_computation | convolution fusion | flops 1610612736 | bytes 6815744 | tf_op jit(solution)/shard_map/fn,rf->nr/dot_general | solution.py:90
  42.0 25.4 %collective-permute-done = bf16[1,512,2048]{2,1,0:T(8,128)(2,1)S(1)} collective-permute-done((bf16[1,512,2048]{2,1,0:T(8,128)(2,1)S(1)}, bf16[1,512,2048]{2,1,0:T(8,128)(2,1)S(1)}, u32[]{:S(2)}, u32[]{:S(2)}) %collective-permute-start) | collective-permute-done | bytes 2097184 | tf_op jit(solution)/shard_map/ppermute | solution.py:58
  67.4 4.9 %fusion.2 = f32[768,512]{1,0:T(8,128)} fusion(bf16[2048,768]{0,1:T(8,128)(2,1)} %bitcast.86, bf16[1,512,2048]{2,1,0:T(8,128)(2,1)S(1)} %collective-permute-done), kind=kOutput, calls=%fused_computation.2 | convolution fusion | flops 1610612736 | bytes 6815744 | tf_op jit(solution)/shard_map/fn,rf->nr/dot_general | solution.py:90
  73.3 11.3 %all-to-all-start.1 = ((f32[32,8,256]{2,1,0:T(8,128)}), f32[32,8,256]{2,1,0:T(8,128)S(1)}, u32[]{:S(2)}, u32[]{:S(2)}) async-start(f32[32,8,256]{2,1,0:T(8,128)} %bitcast.16), calls=%async_computation.3 | async-start | bytes 524288 | tf_op jit(solution)/shard_map/all_to_all | solution.py:78
  84.7 12.3 %all-to-all-done.1 = f32[32,8,256]{2,1,0:T(8,128)S(1)} async-done(((f32[32,8,256]{2,1,0:T(8,128)}), f32[32,8,256]{2,1,0:T(8,128)S(1)}, u32[]{:S(2)}, u32[]{:S(2)}) %all-to-all-start.1) | async-done | bytes 262176 | tf_op jit(solution)/shard_map/all_to_all | solution.py:78
  99.1 1.0 convert_element_type.32
  100.1 5.8 %reduce-scatter.3.cloned.1.call-done = f32[192,512]{1,0:T(8,128)} async-done(((f32[768,512]{1,0:T(8,128)}), f32[192,512]{1,0:T(8,128)}) %reduce-scatter.3.cloned.1.call-update) | async-done | bytes 393232 | tf_op jit(solution)/shard_map/reduce_scatter | solution.py:91
  106.0 1.0 convert_element_type.31
  107.0 0.8 copy.123
  107.8 5.9 %all-to-all-start = ((bf16[8,3,8,1024]{3,2,1,0:T(8,128)(2,1)}), bf16[8,3,8,1024]{3,2,1,0:T(8,128)(2,1)S(1)}, u32[]{:S(2)}, u32[]{:S(2)}) async-start(bf16[8,3,8,1024]{3,2,1,0:T(8,128)(2,1)} %bitcast.83), calls=%async_computation.2 | async-start | bytes 786432 | tf_op jit(solution)/shard_map/all_to_all | solution.py:95
  115.5 12.5 %all-to-all-done = bf16[8,3,8,1024]{3,2,1,0:T(8,128)(2,1)S(1)} async-done(((bf16[8,3,8,1024]{3,2,1,0:T(8,128)(2,1)}), bf16[8,3,8,1024]{3,2,1,0:T(8,128)(2,1)S(1)}, u32[]{:S(2)}, u32[]{:S(2)}) %all-to-all-start) | async-done | bytes 393248 | tf_op jit(solution)/shard_map/all_to_all | solution.py:95
  129.0 1.0 fusion.4
  130.0 1.0 convolution_bitcast_fusion
  131.0 1.8 %fusion.23 = f32[8,128,128]{2,1,0:T(8,128)} fusion(f32[128,128,1]{1,0,2:T(8,128)S(1)} %copy-done.2, f32[8,128,128]{1,2,0:T(8,128)S(1)} %fusion.4, f32[8,128,128]{1,2,0:T(8,128)S(1)} %convolution_bitcast_fusion, f32[128,128]{0,1:T(8,128)S(1)} %copy-done.3, f32[128,128]{0,1:T(8,128)S(1)} %copy-done.4), kind=kOutput, calls=%fused_computation.43 | convolution fusion | flops 201719808 | bytes 1769472 | tf_op jit(solution)/shard_map/ckr,rj->ckj/dot_general | solution.py:40
  132.8 1.0 fusion.24
  133.9 1.8 %copy.91 = f32[1,8,8,1024]{3,2,1,0:T(8,128)} copy(f32[1,8,8,1024]{3,1,0,2:T(8,128)} %slice_convert_fusion) | data formatting | bytes 524288 | tf_op jit(solution)/shard_map/convert_element_type | solution.py:97
  135.7 1.0 reshape.53
  136.7 2.0 %convolution_add_fusion.2 = f32[8,128,128]{2,1,0:T(8,128)S(1)} fusion(f32[8,128,128]{2,1,0:T(8,128)} %fusion.23, f32[128,128,1]{1,0,2:T(8,128)S(1)} %copy-done.5, f32[8,128,128]{1,2,0:T(8,128)S(1)} %convolution_bitcast_fusion, f32[8,128,128]{1,2,0:T(8,128)S(1)} %fusion.4, f32[128,128]{0,1:T(8,128)S(1)} %copy-done.3, f32[128,128]{0,1:T(8,128)S(1)} %copy-done.4), kind=kOutput, calls=%fused_computation.13 | convolution fusion | flops 201850880 | bytes 2293760 | tf_op jit(solution)/shard_map/ckr,rj->ckj/dot_general | solution.py:40
  138.8 1.0 multiply_subtract_fusion.1
  144.1 13.8 %all_to_all.15 = bf16[32,8,256]{2,1,0:T(8,128)(2,1)S(1)} all-to-all(bf16[32,8,256]{2,1,0:T(8,128)(2,1)S(1)} %copy.109), channel_id=1, replica_groups=mesh['section'=8,'seq'=8,'chan'=4] {'seq','chan'}, dimensions={0} | all-to-all | bytes 262144 | tf_op jit(solution)/shard_map/all_to_all | solution.py:108
  157.9 0.8 copy.111
  (63 shorter events, 10.3 us)
Async XLA Ops:
  6.5 78.1 %copy-start = (f32[1,256]{1,0:T(1,128)S(1)}, f32[1,256]{1,0:T(1,128)}, u32[]{:S(2)}) copy-start(f32[1,256]{1,0:T(1,128)} %param.15) | copy-start | bytes 3076
  6.5 92.6 %reduce-scatter.5.cloned.1.call-start = ((), (), s32[]{:S(2)}) async-start(), calls=%async_computation.6 | async-start | bytes 1966080 | tf_op jit(solution)/shard_map/reduce_scatter | solution.py:91
  11.4 25.8 %collective-permute-start.1 = (bf16[1,512,2048]{2,1,0:T(8,128)(2,1)}, bf16[1,512,2048]{2,1,0:T(8,128)(2,1)}, u32[]{:S(2)}, u32[]{:S(2)}) collective-permute-start(bf16[1,512,2048]{2,1,0:T(8,128)(2,1)} %get-tuple-element.6), channel_id=1, source_target_pairs={{0,32},{32,64},{64,96},{96,128},{128,160},{160,192},{192,224},{224... | collective-permute-start | bytes 6291464 | tf_op jit(solution)/shard_map/ppermute | solution.py:58
  14.8 22.4 %copy-start.1 = (bf16[2048,4,3,64]{0,3,2,1:T(8,128)(2,1)}, bf16[2048,4,3,64]{0,3,2,1:T(8,128)(2,1)S(1)}, u32[]{:S(2)}) copy-start(bf16[2048,4,3,64]{0,3,2,1:T(8,128)(2,1)S(1)} %copy.89) | copy-start | bytes 9437188
  37.1 4.8 %copy-start.6 = (bf16[1,512,2048]{2,1,0:T(8,128)(2,1)S(1)}, bf16[1,512,2048]{2,1,0:T(8,128)(2,1)}, u32[]{:S(2)}) copy-start(bf16[1,512,2048]{2,1,0:T(8,128)(2,1)} %get-tuple-element.5) | copy-start | bytes 6291460
  41.9 64.1 %reduce-scatter.3.cloned.1.call-start = ((), (), s32[]{:S(2)}) async-start(), calls=%async_computation.5 | async-start | bytes 1966080 | tf_op jit(solution)/shard_map/reduce_scatter | solution.py:91
  42.0 30.4 %copy-start.9 = (f32[1,256,256]{2,1,0:T(8,128)S(1)}, f32[1,256,256]{2,1,0:T(8,128)}, u32[]{:S(2)}) copy-start(f32[1,256,256]{2,1,0:T(8,128)} %param.14) | copy-start | bytes 786436
  42.0 25.5 %collective-permute-start = (bf16[1,512,2048]{2,1,0:T(8,128)(2,1)S(1)}, bf16[1,512,2048]{2,1,0:T(8,128)(2,1)S(1)}, u32[]{:S(2)}, u32[]{:S(2)}) collective-permute-start(bf16[1,512,2048]{2,1,0:T(8,128)(2,1)S(1)} %copy-done.6), channel_id=1, source_target_pairs={{0,32},{32,64},{64,96},{96,128},{128,160},{160,192},{192,224},{224... | collective-permute-start | bytes 6291464 | tf_op jit(solution)/shard_map/ppermute | solution.py:58
  72.4 24.8 %copy-start.11 = (f32[128,64,1]{0,1,2:T(8,128)S(1)}, f32[128,64,1]{0,1,2:T(8,128)}, u32[]{:S(2)}) copy-start(f32[128,64,1]{0,1,2:T(8,128)} %constant.47) | copy-start | bytes 98308
  72.4 25.4 %copy-start.10 = (f32[128,64,1]{0,1,2:T(8,128)S(1)}, f32[128,64,1]{0,1,2:T(8,128)}, u32[]{:S(2)}) copy-start(f32[128,64,1]{0,1,2:T(8,128)} %constant.46) | copy-start | bytes 98308
  72.4 26.1 %copy-start.2 = (f32[128,128,1]{1,0,2:T(8,128)S(1)}, f32[128,128,1]{1,0,2:T(8,128)}, u32[]{:S(2)}) copy-start(f32[128,128,1]{1,0,2:T(8,128)} %constant.48) | copy-start | bytes 196612
  72.4 26.1 %copy-start.7 = (f32[128,128]{1,0:T(8,128)S(1)}, f32[128,128]{1,0:T(8,128)}, u32[]{:S(2)}) copy-start(f32[128,128]{1,0:T(8,128)} %constant.51) | copy-start | bytes 196612
  72.4 26.1 %copy-start.8 = (f32[128,128]{1,0:T(8,128)S(1)}, f32[128,128]{1,0:T(8,128)}, u32[]{:S(2)}) copy-start(f32[128,128]{1,0:T(8,128)} %constant.50) | copy-start | bytes 196612
  73.3 23.8 %all-to-all-start.1 = ((f32[32,8,256]{2,1,0:T(8,128)}), f32[32,8,256]{2,1,0:T(8,128)S(1)}, u32[]{:S(2)}, u32[]{:S(2)}) async-start(f32[32,8,256]{2,1,0:T(8,128)} %bitcast.16), calls=%async_computation.3 | async-start | bytes 524288 | tf_op jit(solution)/shard_map/all_to_all | solution.py:78
  107.0 7.3 %copy-start.5 = (f32[128,128,1]{1,0,2:T(8,128)S(1)}, f32[128,128,1]{1,0,2:T(8,128)}, u32[]{:S(2)}) copy-start(f32[128,128,1]{1,0,2:T(8,128)} %constant.49) | copy-start | bytes 196612
  107.8 20.2 %all-to-all-start = ((bf16[8,3,8,1024]{3,2,1,0:T(8,128)(2,1)}), bf16[8,3,8,1024]{3,2,1,0:T(8,128)(2,1)S(1)}, u32[]{:S(2)}, u32[]{:S(2)}) async-start(bf16[8,3,8,1024]{3,2,1,0:T(8,128)(2,1)} %bitcast.83), calls=%async_computation.2 | async-start | bytes 786432 | tf_op jit(solution)/shard_map/all_to_all | solution.py:95
  115.5 15.5 %copy-start.3 = (f32[128,128]{0,1:T(8,128)S(1)}, f32[128,128]{0,1:T(8,128)}, u32[]{:S(2)}) copy-start(f32[128,128]{0,1:T(8,128)} %constant.39.clone) | copy-start | bytes 196612
  115.5 15.5 %copy-start.4 = (f32[128,128]{0,1:T(8,128)S(1)}, f32[128,128]{0,1:T(8,128)}, u32[]{:S(2)}) copy-start(f32[128,128]{0,1:T(8,128)} %constant.38.clone) | copy-start | bytes 196612
  140.4 1.9 %copy-start.13 = (f32[128,64,1]{0,1,2:T(8,128)S(1)}, f32[128,64,1]{0,1,2:T(8,128)}, u32[]{:S(2)}) copy-start(f32[128,64,1]{0,1,2:T(8,128)} %constant.52) | copy-start | bytes 98308
  141.1 2.0 %copy-start.12 = (f32[128,64,1]{0,1,2:T(8,128)S(1)}, f32[128,64,1]{0,1,2:T(8,128)}, u32[]{:S(2)}) copy-start(f32[128,64,1]{0,1,2:T(8,128)} %constant.53) | copy-start | bytes 98308
Sparse Core Ops, SparseCore 0:
  42.0 30.9 reduce-scatter.4
  75.6 30.2 reduce-scatter.2

commit v4 on v3

--- a/solution.py
+++ b/solution.py
@@ -8,7 +8,7 @@
 
 
 CHUNKS = 2
-HI = lax.Precision.HIGHEST
+HI = lax.Precision.HIGH
 
 
 def dft_tables(seq_len):
@@ -80,16 +80,17 @@
     taps_re, taps_im = forward(taps, tables)
 
     weight = in_weight[0].reshape(-1, 3, n_chan, chan_width)
-    weight = weight.transpose(0, 2, 1, 3).reshape(-1, 3 * width)
-
+    weight = weight.transpose(0, 2, 1, 3)
+    rows = layer_rows[0]
     pieces = []
-    chunk_rows = seq_rows // CHUNKS
+    piece = chan_width // CHUNKS
     for chunk in range(CHUNKS):
-        rows = layer_rows[:, chunk * chunk_rows : (chunk + 1) * chunk_rows]
-        source = from_behind(rows, "section", 1)[0]
-        partial = jnp.einsum("fn,rf->nr", weight, source, preferred_element_type=jnp.float32)
+        part = weight[:, :, :, chunk * piece : (chunk + 1) * piece].reshape(-1, 3 * n_chan * piece)
+        part = from_behind(part, "section", -1)
+        partial = jnp.einsum("fn,rf->nr", part, rows, preferred_element_type=jnp.float32)
         summed = lax.psum_scatter(partial, "chan", scatter_dimension=0, tiled=True)
-        pieces.append(summed.astype(jnp.bfloat16))
+        summed = summed.astype(jnp.bfloat16).reshape(3, piece, seq_rows)
+        pieces.append(from_behind(summed, "section", 1))
     mixed = jnp.concatenate(pieces, axis=1).reshape(3, n_seq, own, seq_rows)
     mixed = mixed.transpose(1, 0, 2, 3)
     mixed = lax.all_to_all(mixed, "seq", 0, 0, tiled=True)

time: 166 us -> 157 us (0.946)
  matrix products: 25 us -> 18.5 us
  starting transfers between devices: 17.3 us -> 21.1 us
  waiting for transfers between devices: 78.5 us -> 74.9 us
  local copies, waits for them, and re-layouts: 14.2 us -> 10.9 us
    ppermute x2 -> x4, waiting for transfers between devices: 47.8 us -> 40.5 us  [from_behind(): return lax.ppermute(value, axis, pairs)]
    ppermute x2 -> x4, starting transfers between devices: 0.02 us -> 3.35 us  [from_behind(): return lax.ppermute(value, axis, pairs)]
    slice x1 -> x3, local copies, waits for them, and re-layouts: 4.82 us -> 1.63 us  [body(): weight[:, :, :, chunk * piece:(chunk + 1) * piece]]
    reduce_scatter x2, waiting for transfers between devices: 5.85 us -> 8.87 us  [body(): summed = lax.psum_scatter(partial, 'chan', scatter_dimension=0, tiled=True)]
    unnamed x30 -> x32, local copies, waits for them, and re-layouts: 3.4 us -> 6.16 us
    convert_element_type x2, local copies, waits for them, and re-layouts: 2.84 us -> 0.23 us  [body(): queries = mixed[0].astype(jnp.float32)]
  transfers between devices with their start and end apart: 6 -> 8, of which waited for: 5 -> 6; matrix products, arithmetic and copies ran while one was open for 8% -> 7% of each run, Pallas kernels for 0% -> 0%
where the time goes in v4:
time: 157 us; the launch traced here: 156 us
  waiting for transfers between devices  74.9 us (48%)
  starting transfers between devices  21.1 us (13%)
  matrix products  18.5 us (12%)
  between operations  13.8 us (9%)
  blocking collectives  13.6 us (9%)
  local copies, waits for them, and re-layouts  10.9 us (7%)
  other arithmetic  3.13 us (2%)
    ppermute x4, waiting for transfers between devices, from_behind(): return lax.ppermute(value, axis, pairs)  40.5 us
    all_to_all x1, blocking collectives, body(): gated = lax.all_to_all(gated, ('seq', 'chan'), 0, 0, tiled=True)  13.6 us
    all_to_all x1, waiting for transfers between devices, body(): mixed = lax.all_to_all(mixed, 'seq', 0, 0, tiled=True)  12.8 us
    all_to_all x1, waiting for transfers between devices, body(): taps = lax.all_to_all(taps, ('seq', 'chan'), 0, 0, tiled=True)  12.7 us
    all_to_all x1, starting transfers between devices, body(): taps = lax.all_to_all(taps, ('seq', 'chan'), 0, 0, tiled=True)  11.3 us
    reduce_scatter x2, waiting for transfers between devices, body(): summed = lax.psum_scatter(partial, 'chan', scatter_dimension=0, tiled=True)  8.87 us
    dot_general x2, matrix products, body(): jnp.einsum('fn,rf->nr', part, rows, preferred_element_type=jnp.float32)  8.2 us
    all_to_all x1, starting transfers between devices, body(): mixed = lax.all_to_all(mixed, 'seq', 0, 0, tiled=True)  6.37 us
  transfers between devices with their start and end apart: 8, of which 6 were waited for; matrix products, arithmetic and copies ran while one was open for 7% of the time, Pallas kernels for 0%

profile of v4, /device:TPU:8, one launch (start us, length us, event | category | flops | bytes accessed | tf_op | source)
XLA Modules:
  0.0 156.0 jit_solution(2907793683704427321)
XLA Ops:
  6.5 3.2 %copy.136 = bf16[1,2048,768]{1,2,0:T(8,128)(2,1)S(1)} copy(bf16[1,2048,768]{2,1,0:T(8,128)(2,1)} %param.13) | data formatting | bytes 6291456 | tf_op args[1]
  9.8 1.4 fusion.26
  11.3 17.9 %collective-permute-done = bf16[2048,384]{0,1:T(8,128)(2,1)S(1)} collective-permute-done((bf16[2048,384]{0,1:T(8,128)(2,1)S(1)}, bf16[2048,384]{0,1:T(8,128)(2,1)S(1)}, u32[]{:S(2)}, u32[]{:S(2)}) %collective-permute-start) | collective-permute-done | bytes 1572896 | tf_op jit(solution)/shard_map/ppermute | solution.py:58
  29.2 3.0 %fusion.2 = f32[384,1024]{1,0:T(8,128)} fusion(bf16[2048,384]{0,1:T(8,128)(2,1)S(1)} %collective-permute-done, bf16[1,1024,2048]{2,1,0:T(8,128)(2,1)S(1)} %copy-done.14), kind=kOutput, calls=%fused_computation.2 | convolution fusion | flops 1610612736 | bytes 7340032 | tf_op jit(solution)/shard_map/fn,rf->nr/dot_general | solution.py:90
  32.3 1.3 copy-done.1
  33.8 1.9 %collective-permute-start.2 = (bf16[2048,384]{0,1:T(8,128)(2,1)S(1)}, bf16[2048,384]{0,1:T(8,128)(2,1)S(1)}, u32[]{:S(2)}, u32[]{:S(2)}) collective-permute-start(bf16[2048,384]{0,1:T(8,128)(2,1)S(1)} %bitcast.88), channel_id=1, source_target_pairs={{0,224},{32,0},{64,32},{96,64},{128,96},{160,128},{192,160},{224,1... | collective-permute-start | bytes 4718600 | tf_op jit(solution)/shard_map/ppermute | solution.py:58
  35.7 17.9 %collective-permute-done.2 = bf16[2048,384]{0,1:T(8,128)(2,1)S(1)} collective-permute-done((bf16[2048,384]{0,1:T(8,128)(2,1)S(1)}, bf16[2048,384]{0,1:T(8,128)(2,1)S(1)}, u32[]{:S(2)}, u32[]{:S(2)}) %collective-permute-start.2) | collective-permute-done | bytes 1572896 | tf_op jit(solution)/shard_map/ppermute | solution.py:58
  53.6 5.2 %fusion = f32[384,1024]{1,0:T(8,128)} fusion(bf16[2048,384]{0,1:T(8,128)(2,1)S(1)} %collective-permute-done.2, bf16[1,1024,2048]{2,1,0:T(8,128)(2,1)} %param.12), kind=kOutput, calls=%fused_computation | convolution fusion | flops 1610612736 | bytes 7340032 | tf_op jit(solution)/shard_map/fn,rf->nr/dot_general | solution.py:90
  58.8 0.9 copy-done.9
  60.6 11.3 %all-to-all-start.1 = ((f32[32,8,256]{2,1,0:T(8,128)}), f32[32,8,256]{2,1,0:T(8,128)S(1)}, u32[]{:S(2)}, u32[]{:S(2)}) async-start(f32[32,8,256]{2,1,0:T(8,128)} %bitcast.19), calls=%async_computation.3 | async-start | bytes 524288 | tf_op jit(solution)/shard_map/all_to_all | solution.py:78
  72.1 12.7 %all-to-all-done.1 = f32[32,8,256]{2,1,0:T(8,128)S(1)} async-done(((f32[32,8,256]{2,1,0:T(8,128)}), f32[32,8,256]{2,1,0:T(8,128)S(1)}, u32[]{:S(2)}, u32[]{:S(2)}) %all-to-all-start.1) | async-done | bytes 262176 | tf_op jit(solution)/shard_map/all_to_all | solution.py:78
  85.8 1.0 convert_element_type.31
  86.9 1.4 collective-permute-start.1
  88.3 8.8 %reduce-scatter.5.cloned.1.call-done = f32[96,1024]{1,0:T(8,128)} async-done(((f32[384,1024]{1,0:T(8,128)}), f32[96,1024]{1,0:T(8,128)}) %reduce-scatter.5.cloned.1.call-update) | async-done | bytes 393232 | tf_op jit(solution)/shard_map/reduce_scatter | solution.py:91
  97.1 1.0 convert_element_type.32
  98.6 4.7 %collective-permute-done.3 = bf16[3,32,1024]{2,1,0:T(8,128)(2,1)S(1)} collective-permute-done((bf16[3,32,1024]{2,1,0:T(8,128)(2,1)S(1)}, bf16[3,32,1024]{2,1,0:T(8,128)(2,1)S(1)}, u32[]{:S(2)}, u32[]{:S(2)}) %collective-permute-start.3) | collective-permute-done | bytes 196640 | tf_op jit(solution)/shard_map/ppermute | solution.py:58
  103.3 0.8 copy.139
  104.0 6.4 %all-to-all-start = ((bf16[8,3,8,1024]{3,2,1,0:T(8,128)(2,1)}), bf16[8,3,8,1024]{3,2,1,0:T(8,128)(2,1)S(1)}, u32[]{:S(2)}, u32[]{:S(2)}) async-start(bf16[8,3,8,1024]{3,2,1,0:T(8,128)(2,1)} %copy.139), calls=%async_computation.2 | async-start | bytes 786432 | tf_op jit(solution)/shard_map/all_to_all | solution.py:96
  111.6 12.8 %all-to-all-done = bf16[8,3,8,1024]{3,2,1,0:T(8,128)(2,1)S(1)} async-done(((bf16[8,3,8,1024]{3,2,1,0:T(8,128)(2,1)}), bf16[8,3,8,1024]{3,2,1,0:T(8,128)(2,1)S(1)}, u32[]{:S(2)}, u32[]{:S(2)}) %all-to-all-start) | async-done | bytes 393248 | tf_op jit(solution)/shard_map/all_to_all | solution.py:96
  126.3 1.4 fusion.23
  128.4 0.9 slice_convert_fusion
  129.3 1.6 %convolution_add_fusion.2 = f32[8,128,128]{2,1,0:T(8,128)S(1)} fusion(f32[8,128,128]{2,1,0:T(8,128)} %fusion.23, f32[128,128,1]{1,0,2:T(8,128)S(1)} %copy-done.5, f32[8,128,128]{1,2,0:T(8,128)S(1)} %convolution_bitcast_fusion, f32[8,128,128]{1,2,0:T(8,128)S(1)} %fusion.4, f32[128,128]{0,1:T(8,128)S(1)} %copy-done.4, f32[128,128]{0,1:T(8,128)S(1)} %copy-done.3), kind=kOutput, calls=%fused_computation.13 | convolution fusion | flops 101187584 | bytes 2293760 | tf_op jit(solution)/shard_map/ckr,rj->ckj/dot_general | solution.py:40
  134.7 13.6 %all_to_all.15 = bf16[32,8,256]{2,1,0:T(8,128)(2,1)S(1)} all-to-all(bf16[32,8,256]{2,1,0:T(8,128)(2,1)S(1)} %copy.158), channel_id=1, replica_groups=mesh['section'=8,'seq'=8,'chan'=4] {'seq','chan'}, dimensions={0} | all-to-all | bytes 262144 | tf_op jit(solution)/shard_map/all_to_all | solution.py:109
  148.4 0.8 copy.160
  (70 shorter events, 10.1 us)
Async XLA Ops:
  6.5 65.4 %copy-start = (f32[1,256]{1,0:T(1,128)S(1)}, f32[1,256]{1,0:T(1,128)}, u32[]{:S(2)}) copy-start(f32[1,256]{1,0:T(1,128)} %param.15) | copy-start | bytes 3076
  6.5 79.3 %reduce-scatter.3.cloned.1.call-start = ((), (), s32[]{:S(2)}) async-start(), calls=%async_computation.5 | async-start | bytes 1966080 | tf_op jit(solution)/shard_map/reduce_scatter | solution.py:91
  9.7 19.4 %copy-start.14 = (bf16[1,1024,2048]{2,1,0:T(8,128)(2,1)S(1)}, bf16[1,1024,2048]{2,1,0:T(8,128)(2,1)}, u32[]{:S(2)}) copy-start(bf16[1,1024,2048]{2,1,0:T(8,128)(2,1)} %param.12) | copy-start | bytes 12582916
  11.2 18.0 %collective-permute-start = (bf16[2048,384]{0,1:T(8,128)(2,1)S(1)}, bf16[2048,384]{0,1:T(8,128)(2,1)S(1)}, u32[]{:S(2)}, u32[]{:S(2)}) collective-permute-start(bf16[2048,384]{0,1:T(8,128)(2,1)S(1)} %bitcast.87), channel_id=1, source_target_pairs={{0,224},{32,0},{64,32},{96,64},{128,96},{160,128},{192,160},{224,1... | collective-permute-start | bytes 4718600 | tf_op jit(solution)/shard_map/ppermute | solution.py:58
  32.2 1.4 copy-start.1
  32.2 64.9 %reduce-scatter.5.cloned.1.call-start = ((), (), s32[]{:S(2)}) async-start(), calls=%async_computation.6 | async-start | bytes 1966080 | tf_op jit(solution)/shard_map/reduce_scatter | solution.py:91
  33.8 19.9 %collective-permute-start.2 = (bf16[2048,384]{0,1:T(8,128)(2,1)S(1)}, bf16[2048,384]{0,1:T(8,128)(2,1)S(1)}, u32[]{:S(2)}, u32[]{:S(2)}) collective-permute-start(bf16[2048,384]{0,1:T(8,128)(2,1)S(1)} %bitcast.88), channel_id=1, source_target_pairs={{0,224},{32,0},{64,32},{96,64},{128,96},{160,128},{192,160},{224,1... | collective-permute-start | bytes 4718600 | tf_op jit(solution)/shard_map/ppermute | solution.py:58
  58.8 0.9 copy-start.9
  59.8 25.2 %copy-start.10 = (f32[128,64,1]{0,1,2:T(8,128)S(1)}, f32[128,64,1]{0,1,2:T(8,128)}, u32[]{:S(2)}) copy-start(f32[128,64,1]{0,1,2:T(8,128)} %constant.47) | copy-start | bytes 98308
  59.9 25.5 %copy-start.11 = (f32[128,64,1]{0,1,2:T(8,128)S(1)}, f32[128,64,1]{0,1,2:T(8,128)}, u32[]{:S(2)}) copy-start(f32[128,64,1]{0,1,2:T(8,128)} %constant.46) | copy-start | bytes 98308
  60.6 24.2 %all-to-all-start.1 = ((f32[32,8,256]{2,1,0:T(8,128)}), f32[32,8,256]{2,1,0:T(8,128)S(1)}, u32[]{:S(2)}, u32[]{:S(2)}) async-start(f32[32,8,256]{2,1,0:T(8,128)} %bitcast.19), calls=%async_computation.3 | async-start | bytes 524288 | tf_op jit(solution)/shard_map/all_to_all | solution.py:78
  84.9 13.3 %copy-start.2 = (f32[128,128,1]{1,0,2:T(8,128)S(1)}, f32[128,128,1]{1,0,2:T(8,128)}, u32[]{:S(2)}) copy-start(f32[128,128,1]{1,0,2:T(8,128)} %constant.48) | copy-start | bytes 196612
  84.9 13.3 %copy-start.7 = (f32[128,128]{1,0:T(8,128)S(1)}, f32[128,128]{1,0:T(8,128)}, u32[]{:S(2)}) copy-start(f32[128,128]{1,0:T(8,128)} %constant.50) | copy-start | bytes 196612
  84.9 13.3 %copy-start.8 = (f32[128,128]{1,0:T(8,128)S(1)}, f32[128,128]{1,0:T(8,128)}, u32[]{:S(2)}) copy-start(f32[128,128]{1,0:T(8,128)} %constant.51) | copy-start | bytes 196612
  86.9 11.7 %collective-permute-start.1 = (bf16[3,32,1024]{2,1,0:T(8,128)(2,1)S(1)}, bf16[3,32,1024]{2,1,0:T(8,128)(2,1)S(1)}, u32[]{:S(2)}, u32[]{:S(2)}) collective-permute-start(bf16[3,32,1024]{2,1,0:T(8,128)(2,1)S(1)} %bitcast.95), channel_id=1, source_target_pairs={{0,32},{32,64},{64,96},{96,128},{128,160},{160,192},{192,224},{224... | collective-permute-start | bytes 589832 | tf_op jit(solution)/shard_map/ppermute | solution.py:58
  98.1 5.1 %collective-permute-start.3 = (bf16[3,32,1024]{2,1,0:T(8,128)(2,1)S(1)}, bf16[3,32,1024]{2,1,0:T(8,128)(2,1)S(1)}, u32[]{:S(2)}, u32[]{:S(2)}) collective-permute-start(bf16[3,32,1024]{2,1,0:T(8,128)(2,1)S(1)} %bitcast.96), channel_id=1, source_target_pairs={{0,32},{32,64},{64,96},{96,128},{128,160},{160,192},{192,224},{224... | collective-permute-start | bytes 589832 | tf_op jit(solution)/shard_map/ppermute | solution.py:58
  103.3 7.5 %copy-start.5 = (f32[128,128,1]{1,0,2:T(8,128)S(1)}, f32[128,128,1]{1,0,2:T(8,128)}, u32[]{:S(2)}) copy-start(f32[128,128,1]{1,0,2:T(8,128)} %constant.49) | copy-start | bytes 196612
  104.0 20.3 %all-to-all-start = ((bf16[8,3,8,1024]{3,2,1,0:T(8,128)(2,1)}), bf16[8,3,8,1024]{3,2,1,0:T(8,128)(2,1)S(1)}, u32[]{:S(2)}, u32[]{:S(2)}) async-start(bf16[8,3,8,1024]{3,2,1,0:T(8,128)(2,1)} %copy.139), calls=%async_computation.2 | async-start | bytes 786432 | tf_op jit(solution)/shard_map/all_to_all | solution.py:96
  124.3 0.8 copy-start.6
  124.3 2.0 %copy-start.3 = (f32[128,128]{0,1:T(8,128)S(1)}, f32[128,128]{0,1:T(8,128)}, u32[]{:S(2)}) copy-start(f32[128,128]{0,1:T(8,128)} %constant.38.clone) | copy-start | bytes 196612
  124.3 2.0 %copy-start.4 = (f32[128,128]{0,1:T(8,128)S(1)}, f32[128,128]{0,1:T(8,128)}, u32[]{:S(2)}) copy-start(f32[128,128]{0,1:T(8,128)} %constant.39.clone) | copy-start | bytes 196612
  132.4 0.9 copy-start.13
  132.9 0.9 copy-start.12
Sparse Core Ops, SparseCore 0:
  32.3 33.4 reduce-scatter.2
  68.4 28.6 reduce-scatter.4

commit v5 on v4

--- a/solution.py
+++ b/solution.py
@@ -58,6 +58,17 @@
     return lax.ppermute(value, axis, pairs)
 
 
+def to_owner(value, shift):
+    sections = lax.axis_size("section")
+    count = lax.axis_size("seq")
+    pairs = [
+        (s * count + q, ((s + 1) % sections) * count + (q + shift) % count)
+        for s in range(sections)
+        for q in range(count)
+    ]
+    return lax.ppermute(value, ("section", "seq"), pairs)
+
+
 def body(layer_rows, in_weight, long_filter, skip_gain):
     n_chan = lax.axis_size("chan")
     n_seq = lax.axis_size("seq")
@@ -79,22 +90,26 @@
     taps = taps.reshape(n_pos, own, block_rows).transpose(1, 0, 2).reshape(own, seq_len)
     taps_re, taps_im = forward(taps, tables)
 
-    weight = in_weight[0].reshape(-1, 3, n_chan, chan_width)
-    weight = weight.transpose(0, 2, 1, 3)
+    weight = in_weight[0].reshape(-1, 3, n_chan, n_seq, own)
+    weight = jnp.concatenate([weight, weight], axis=3)
+    weight = lax.dynamic_slice_in_dim(weight, q_index, n_seq, axis=3)
+    weight = weight.transpose(0, 2, 1, 3, 4)
     rows = layer_rows[0]
-    pieces = []
-    piece = chan_width // CHUNKS
+    arrived = [None] * n_seq
+    shifts = n_seq // CHUNKS
     for chunk in range(CHUNKS):
-        part = weight[:, :, :, chunk * piece : (chunk + 1) * piece].reshape(-1, 3 * n_chan * piece)
+        part = weight[:, :, :, chunk * shifts : (chunk + 1) * shifts].reshape(-1, 3 * n_chan * shifts * own)
         part = from_behind(part, "section", -1)
         partial = jnp.einsum("fn,rf->nr", part, rows, preferred_element_type=jnp.float32)
         summed = lax.psum_scatter(partial, "chan", scatter_dimension=0, tiled=True)
-        summed = summed.astype(jnp.bfloat16).reshape(3, piece, seq_rows)
-        pieces.append(from_behind(summed, "section", 1))
-    mixed = jnp.concatenate(pieces, axis=1).reshape(3, n_seq, own, seq_rows)
-    mixed = mixed.transpose(1, 0, 2, 3)
-    mixed = lax.all_to_all(mixed, "seq", 0, 0, tiled=True)
-    mixed = mixed.reshape(n_seq, 3, own, seq_rows).transpose(1, 2, 0, 3).reshape(3, own, seq_len)
+        summed = summed.astype(jnp.bfloat16).reshape(3, shifts, own, seq_rows)
+        for step in range(shifts):
+            shift = chunk * shifts + step
+            arrived[shift] = to_owner(summed[:, step], shift)
+    stacked = jnp.stack(arrived[::-1])
+    stacked = jnp.concatenate([stacked, stacked], axis=0)
+    mixed = lax.dynamic_slice_in_dim(stacked, n_seq - 1 - q_index, n_seq, axis=0)
+    mixed = mixed.transpose(1, 2, 0, 3).reshape(3, own, seq_len)
     queries = mixed[0].astype(jnp.float32)
     signal = mixed[1].astype(jnp.float32) * mixed[2].astype(jnp.float32)
 

time: 157 us -> 146 us (0.930)
  waiting for transfers between devices: 74.9 us -> 54.4 us
  starting transfers between devices: 21.1 us -> 30.2 us
  blocking collectives: 13.6 us -> 16.7 us
  local copies, waits for them, and re-layouts: 10.9 us -> 8.24 us
    ppermute x0 -> x8, starting transfers between devices: none -> 16.7 us  [to_owner(): return lax.ppermute(value, ('section', 'seq'), pairs)]
    all_to_all x1 -> x0, waiting for transfers between devices: 12.8 us -> none  [body(): mixed = lax.all_to_all(mixed, 'seq', 0, 0, tiled=True)]
    reduce_scatter x2, waiting for transfers between devices: 8.87 us -> 1.17 us  [body(): summed = lax.psum_scatter(partial, 'chan', scatter_dimension=0, tiled=True)]
    all_to_all x1 -> x0, starting transfers between devices: 6.37 us -> none  [body(): mixed = lax.all_to_all(mixed, 'seq', 0, 0, tiled=True)]
    ppermute x4 -> x2, waiting for transfers between devices: 40.5 us -> 35.9 us  [from_behind(): return lax.ppermute(value, axis, pairs)]
    ppermute x0 -> x8, waiting for transfers between devices: none -> 4.62 us  [to_owner(): return lax.ppermute(value, ('section', 'seq'), pairs)]
    all_to_all x1, blocking collectives: 13.6 us -> 16.7 us  [body(): gated = lax.all_to_all(gated, ('seq', 'chan'), 0, 0, tiled=True)]
    unnamed x32 -> x45, local copies, waits for them, and re-layouts: 6.16 us -> 4.61 us
  transfers between devices with their start and end apart: 8 -> 13, of which waited for: 6 -> 7; matrix products, arithmetic and copies ran while one was open for 7% -> 7% of each run, Pallas kernels for 0% -> 0%
where the time goes in v5:
time: 146 us; the launch traced here: 145 us
  waiting for transfers between devices  54.4 us (37%)
  starting transfers between devices  30.2 us (21%)
  matrix products  18.6 us (13%)
  blocking collectives  16.7 us (11%)
  between operations  14 us (10%)
  local copies, waits for them, and re-layouts  8.24 us (6%)
  other arithmetic  3.33 us (2%)
    ppermute x2, waiting for transfers between devices, from_behind(): return lax.ppermute(value, axis, pairs)  35.9 us
    ppermute x8, starting transfers between devices, to_owner(): return lax.ppermute(value, ('section', 'seq'), pairs)  16.7 us
    all_to_all x1, blocking collectives, body(): gated = lax.all_to_all(gated, ('seq', 'chan'), 0, 0, tiled=True)  16.7 us
    all_to_all x1, waiting for transfers between devices, body(): taps = lax.all_to_all(taps, ('seq', 'chan'), 0, 0, tiled=True)  12.7 us
    all_to_all x1, starting transfers between devices, body(): taps = lax.all_to_all(taps, ('seq', 'chan'), 0, 0, tiled=True)  11.5 us
    dot_general x2, matrix products, body(): jnp.einsum('fn,rf->nr', part, rows, preferred_element_type=jnp.float32)  8.18 us
    ppermute x8, waiting for transfers between devices, to_owner(): return lax.ppermute(value, ('section', 'seq'), pairs)  4.62 us
    unnamed x45, local copies, waits for them, and re-layouts  4.61 us
  transfers between devices with their start and end apart: 13, of which 7 were waited for; matrix products, arithmetic and copies ran while one was open for 7% of the time, Pallas kernels for 0%

profile of v5, /device:TPU:8, one launch (start us, length us, event | category | flops | bytes accessed | tf_op | source)
XLA Modules:
  0.0 145.4 jit_solution(14114143046202489941)
XLA Ops:
  6.5 3.2 %copy.153 = bf16[1,2048,768]{1,2,0:T(8,128)(2,1)S(1)} copy(bf16[1,2048,768]{2,1,0:T(8,128)(2,1)} %param.13) | data formatting | bytes 6291456 | tf_op args[1]
  9.7 1.1 fusion.5
  11.3 17.9 %collective-permute-done = bf16[2048,384]{0,1:T(8,128)(2,1)S(1)} collective-permute-done((bf16[2048,384]{0,1:T(8,128)(2,1)S(1)}, bf16[2048,384]{0,1:T(8,128)(2,1)S(1)}, u32[]{:S(2)}, u32[]{:S(2)}) %collective-permute-start) | collective-permute-done | bytes 1572896 | tf_op jit(solution)/shard_map/ppermute | solution.py:58
  29.2 3.0 %fusion.2 = f32[384,1024]{1,0:T(8,128)} fusion(bf16[2048,384]{0,1:T(8,128)(2,1)S(1)} %collective-permute-done, bf16[1,1024,2048]{2,1,0:T(8,128)(2,1)S(1)} %copy-done.13), kind=kOutput, calls=%fused_computation.4 | convolution fusion | flops 1610612736 | bytes 7340032 | tf_op jit(solution)/shard_map/fn,rf->nr/dot_general | solution.py:103
  32.5 1.9 %collective-permute-start.5 = (bf16[2048,384]{0,1:T(8,128)(2,1)S(1)}, bf16[2048,384]{0,1:T(8,128)(2,1)S(1)}, u32[]{:S(2)}, u32[]{:S(2)}) collective-permute-start(bf16[2048,384]{0,1:T(8,128)(2,1)S(1)} %bitcast.141), channel_id=1, source_target_pairs={{0,224},{32,0},{64,32},{96,64},{128,96},{160,128},{192,160},{224,1... | collective-permute-start | bytes 4718600 | tf_op jit(solution)/shard_map/ppermute | solution.py:58
  34.4 17.9 %collective-permute-done.5 = bf16[2048,384]{0,1:T(8,128)(2,1)S(1)} collective-permute-done((bf16[2048,384]{0,1:T(8,128)(2,1)S(1)}, bf16[2048,384]{0,1:T(8,128)(2,1)S(1)}, u32[]{:S(2)}, u32[]{:S(2)}) %collective-permute-start.5) | collective-permute-done | bytes 1572896 | tf_op jit(solution)/shard_map/ppermute | solution.py:58
  52.3 5.1 %fusion = f32[384,1024]{1,0:T(8,128)} fusion(bf16[2048,384]{0,1:T(8,128)(2,1)S(1)} %collective-permute-done.5, bf16[1,1024,2048]{2,1,0:T(8,128)(2,1)} %param.12), kind=kOutput, calls=%fused_computation.2 | convolution fusion | flops 1610612736 | bytes 7340032 | tf_op jit(solution)/shard_map/fn,rf->nr/dot_general | solution.py:103
  59.3 11.5 %all-to-all-start = ((f32[32,8,256]{2,1,0:T(8,128)}), f32[32,8,256]{2,1,0:T(8,128)S(1)}, u32[]{:S(2)}, u32[]{:S(2)}) async-start(f32[32,8,256]{2,1,0:T(8,128)} %bitcast.32), calls=%async_computation.2 | async-start | bytes 524288 | tf_op jit(solution)/shard_map/all_to_all | solution.py:89
  70.9 12.7 %all-to-all-done = f32[32,8,256]{2,1,0:T(8,128)S(1)} async-done(((f32[32,8,256]{2,1,0:T(8,128)}), f32[32,8,256]{2,1,0:T(8,128)S(1)}, u32[]{:S(2)}, u32[]{:S(2)}) %all-to-all-start) | async-done | bytes 262176 | tf_op jit(solution)/shard_map/all_to_all | solution.py:89
  86.3 1.0 convert_element_type.31
  87.4 1.5 %collective-permute-start.1 = (bf16[3,8,1024]{2,1,0:T(8,128)(2,1)S(1)}, bf16[3,8,1024]{2,1,0:T(8,128)(2,1)S(1)}, u32[]{:S(2)}, u32[]{:S(2)}) collective-permute-start(bf16[3,8,1024]{2,1,0:T(8,128)(2,1)S(1)} %get-tuple-element.16), channel_id=1, source_target_pairs={{0,60},{4,32},{8,36},{12,40},{16,44},{20,48},{24,52},{28,56},{32,9... | collective-permute-start | bytes 147464 | tf_op jit(solution)/shard_map/ppermute | solution.py:69
  88.8 1.4 collective-permute-start.2
  90.2 4.2 %collective-permute-start.3 = (bf16[3,8,1024]{2,1,0:T(8,128)(2,1)S(1)}, bf16[3,8,1024]{2,1,0:T(8,128)(2,1)S(1)}, u32[]{:S(2)}, u32[]{:S(2)}) collective-permute-start(bf16[3,8,1024]{2,1,0:T(8,128)(2,1)S(1)} %get-tuple-element.14), channel_id=1, source_target_pairs={{0,52},{4,56},{8,60},{12,32},{16,36},{20,40},{24,44},{28,48},{32,8... | collective-permute-start | bytes 147464 | tf_op jit(solution)/shard_map/ppermute | solution.py:69
  94.4 1.3 collective-permute-start.4
  95.7 1.2 reduce-scatter.5.cloned.1.call-done
  97.9 3.0 %collective-permute-start.6 = (bf16[3,8,1024]{2,1,0:T(8,128)(2,1)S(1)}, bf16[3,8,1024]{2,1,0:T(8,128)(2,1)S(1)}, u32[]{:S(2)}, u32[]{:S(2)}) collective-permute-start(bf16[3,8,1024]{2,1,0:T(8,128)(2,1)S(1)} %get-tuple-element.12), channel_id=1, source_target_pairs={{0,44},{4,48},{8,52},{12,56},{16,60},{20,32},{24,36},{28,40},{32,7... | collective-permute-start | bytes 147464 | tf_op jit(solution)/shard_map/ppermute | solution.py:69
  101.0 3.8 %collective-permute-start.7 = (bf16[3,8,1024]{2,1,0:T(8,128)(2,1)S(1)}, bf16[3,8,1024]{2,1,0:T(8,128)(2,1)S(1)}, u32[]{:S(2)}, u32[]{:S(2)}) collective-permute-start(bf16[3,8,1024]{2,1,0:T(8,128)(2,1)S(1)} %get-tuple-element.11), channel_id=1, source_target_pairs={{0,40},{4,44},{8,48},{12,52},{16,56},{20,60},{24,32},{28,36},{32,7... | collective-permute-start | bytes 147464 | tf_op jit(solution)/shard_map/ppermute | solution.py:69
  104.9 1.4 collective-permute-start.9
  106.3 1.5 %collective-permute-done.6 = bf16[3,8,1024]{2,1,0:T(8,128)(2,1)S(1)} collective-permute-done((bf16[3,8,1024]{2,1,0:T(8,128)(2,1)S(1)}, bf16[3,8,1024]{2,1,0:T(8,128)(2,1)S(1)}, u32[]{:S(2)}, u32[]{:S(2)}) %collective-permute-start.6) | collective-permute-done | bytes 49184 | tf_op jit(solution)/shard_map/ppermute | solution.py:69
  107.8 1.2 collective-permute-done.7
  109.1 1.9 %collective-permute-done.8 = bf16[3,8,1024]{2,1,0:T(8,128)(2,1)S(1)} collective-permute-done((bf16[3,8,1024]{2,1,0:T(8,128)(2,1)S(1)}, bf16[3,8,1024]{2,1,0:T(8,128)(2,1)S(1)}, u32[]{:S(2)}, u32[]{:S(2)}) %collective-permute-start.8) | collective-permute-done | bytes 49184 | tf_op jit(solution)/shard_map/ppermute | solution.py:69
  113.3 1.4 fusion.25
  115.5 1.6 %convolution_add_fusion.2 = f32[8,128,128]{2,1,0:T(8,128)S(1)} fusion(f32[8,128,128]{2,1,0:T(8,128)} %fusion.25, f32[128,128,1]{1,0,2:T(8,128)S(1)} %copy-done.4, f32[8,128,128]{1,2,0:T(8,128)S(1)} %convolution_bitcast_fusion, f32[8,128,128]{1,2,0:T(8,128)S(1)} %fusion.6, f32[128,128]{0,1:T(8,128)S(1)} %copy-done.3, f32[128,128]{0,1:T(8,128)S(1)} %copy-done.2), kind=kOutput, calls=%fused_computation.17 | convolution fusion | flops 101187584 | bytes 2293760 | tf_op jit(solution)/shard_map/ckr,rj->ckj/dot_general | solution.py:40
  121.1 16.7 %all_to_all.10 = bf16[32,8,256]{2,1,0:T(8,128)(2,1)S(1)} all-to-all(bf16[32,8,256]{2,1,0:T(8,128)(2,1)S(1)} %copy.182), channel_id=1, replica_groups=mesh['section'=8,'seq'=8,'chan'=4] {'seq','chan'}, dimensions={0} | all-to-all | bytes 262144 | tf_op jit(solution)/shard_map/all_to_all | solution.py:124
  (96 shorter events, 13.7 us)
Async XLA Ops:
  6.5 64.3 %copy-start = (f32[1,256]{1,0:T(1,128)S(1)}, f32[1,256]{1,0:T(1,128)}, u32[]{:S(2)}) copy-start(f32[1,256]{1,0:T(1,128)} %param.15) | copy-start | bytes 3076
  6.5 79.8 %reduce-scatter.3.cloned.1.call-start = ((), (), s32[]{:S(2)}) async-start(), calls=%async_computation.4 | async-start | bytes 1966080 | tf_op jit(solution)/shard_map/reduce_scatter | solution.py:104
  10.9 18.3 %copy-start.13 = (bf16[1,1024,2048]{2,1,0:T(8,128)(2,1)S(1)}, bf16[1,1024,2048]{2,1,0:T(8,128)(2,1)}, u32[]{:S(2)}) copy-start(bf16[1,1024,2048]{2,1,0:T(8,128)(2,1)} %param.12) | copy-start | bytes 12582916
  11.2 18.0 %collective-permute-start = (bf16[2048,384]{0,1:T(8,128)(2,1)S(1)}, bf16[2048,384]{0,1:T(8,128)(2,1)S(1)}, u32[]{:S(2)}, u32[]{:S(2)}) collective-permute-start(bf16[2048,384]{0,1:T(8,128)(2,1)S(1)} %bitcast.140), channel_id=1, source_target_pairs={{0,224},{32,0},{64,32},{96,64},{128,96},{160,128},{192,160},{224,1... | collective-permute-start | bytes 4718600 | tf_op jit(solution)/shard_map/ppermute | solution.py:58
  32.2 64.6 %reduce-scatter.5.cloned.1.call-start = ((), (), s32[]{:S(2)}) async-start(), calls=%async_computation.5 | async-start | bytes 1966080 | tf_op jit(solution)/shard_map/reduce_scatter | solution.py:104
  32.5 19.9 %collective-permute-start.5 = (bf16[2048,384]{0,1:T(8,128)(2,1)S(1)}, bf16[2048,384]{0,1:T(8,128)(2,1)S(1)}, u32[]{:S(2)}, u32[]{:S(2)}) collective-permute-start(bf16[2048,384]{0,1:T(8,128)(2,1)S(1)} %bitcast.141), channel_id=1, source_target_pairs={{0,224},{32,0},{64,32},{96,64},{128,96},{160,128},{192,160},{224,1... | collective-permute-start | bytes 4718600 | tf_op jit(solution)/shard_map/ppermute | solution.py:58
  57.5 1.0 copy-start.8
  58.4 25.3 %copy-start.9 = (f32[128,64,1]{0,1,2:T(8,128)S(1)}, f32[128,64,1]{0,1,2:T(8,128)}, u32[]{:S(2)}) copy-start(f32[128,64,1]{0,1,2:T(8,128)} %constant.53) | copy-start | bytes 98308
  58.6 25.6 %copy-start.10 = (f32[128,64,1]{0,1,2:T(8,128)S(1)}, f32[128,64,1]{0,1,2:T(8,128)}, u32[]{:S(2)}) copy-start(f32[128,64,1]{0,1,2:T(8,128)} %constant.52) | copy-start | bytes 98308
  59.3 25.3 %copy-start.1 = (f32[128,128,1]{1,0,2:T(8,128)S(1)}, f32[128,128,1]{1,0,2:T(8,128)}, u32[]{:S(2)}) copy-start(f32[128,128,1]{1,0,2:T(8,128)} %constant.54) | copy-start | bytes 196612
  59.3 25.3 %copy-start.5 = (f32[128,128]{1,0:T(8,128)S(1)}, f32[128,128]{1,0:T(8,128)}, u32[]{:S(2)}) copy-start(f32[128,128]{1,0:T(8,128)} %constant.56) | copy-start | bytes 196612
  59.3 25.3 %copy-start.6 = (f32[128,128]{1,0:T(8,128)S(1)}, f32[128,128]{1,0:T(8,128)}, u32[]{:S(2)}) copy-start(f32[128,128]{1,0:T(8,128)} %constant.57) | copy-start | bytes 196612
  59.3 24.3 %all-to-all-start = ((f32[32,8,256]{2,1,0:T(8,128)}), f32[32,8,256]{2,1,0:T(8,128)S(1)}, u32[]{:S(2)}, u32[]{:S(2)}) async-start(f32[32,8,256]{2,1,0:T(8,128)} %bitcast.32), calls=%async_computation.2 | async-start | bytes 524288 | tf_op jit(solution)/shard_map/all_to_all | solution.py:89
  87.4 13.6 %collective-permute-start.1 = (bf16[3,8,1024]{2,1,0:T(8,128)(2,1)S(1)}, bf16[3,8,1024]{2,1,0:T(8,128)(2,1)S(1)}, u32[]{:S(2)}, u32[]{:S(2)}) collective-permute-start(bf16[3,8,1024]{2,1,0:T(8,128)(2,1)S(1)} %get-tuple-element.16), channel_id=1, source_target_pairs={{0,60},{4,32},{8,36},{12,40},{16,44},{20,48},{24,52},{28,56},{32,9... | collective-permute-start | bytes 147464 | tf_op jit(solution)/shard_map/ppermute | solution.py:69
  88.8 16.0 %collective-permute-start.2 = (bf16[3,8,1024]{2,1,0:T(8,128)(2,1)S(1)}, bf16[3,8,1024]{2,1,0:T(8,128)(2,1)S(1)}, u32[]{:S(2)}, u32[]{:S(2)}) collective-permute-start(bf16[3,8,1024]{2,1,0:T(8,128)(2,1)S(1)} %get-tuple-element.15), channel_id=1, source_target_pairs={{0,56},{4,60},{8,32},{12,36},{16,40},{20,44},{24,48},{28,52},{32,8... | collective-permute-start | bytes 147464 | tf_op jit(solution)/shard_map/ppermute | solution.py:69
  90.2 14.7 %collective-permute-start.3 = (bf16[3,8,1024]{2,1,0:T(8,128)(2,1)S(1)}, bf16[3,8,1024]{2,1,0:T(8,128)(2,1)S(1)}, u32[]{:S(2)}, u32[]{:S(2)}) collective-permute-start(bf16[3,8,1024]{2,1,0:T(8,128)(2,1)S(1)} %get-tuple-element.14), channel_id=1, source_target_pairs={{0,52},{4,56},{8,60},{12,32},{16,36},{20,40},{24,44},{28,48},{32,8... | collective-permute-start | bytes 147464 | tf_op jit(solution)/shard_map/ppermute | solution.py:69
  94.4 11.9 %collective-permute-start.4 = (bf16[3,8,1024]{2,1,0:T(8,128)(2,1)S(1)}, bf16[3,8,1024]{2,1,0:T(8,128)(2,1)S(1)}, u32[]{:S(2)}, u32[]{:S(2)}) collective-permute-start(bf16[3,8,1024]{2,1,0:T(8,128)(2,1)S(1)} %get-tuple-element.13), channel_id=1, source_target_pairs={{0,48},{4,52},{8,56},{12,60},{16,32},{20,36},{24,40},{28,44},{32,8... | collective-permute-start | bytes 147464 | tf_op jit(solution)/shard_map/ppermute | solution.py:69
  97.9 9.9 %collective-permute-start.6 = (bf16[3,8,1024]{2,1,0:T(8,128)(2,1)S(1)}, bf16[3,8,1024]{2,1,0:T(8,128)(2,1)S(1)}, u32[]{:S(2)}, u32[]{:S(2)}) collective-permute-start(bf16[3,8,1024]{2,1,0:T(8,128)(2,1)S(1)} %get-tuple-element.12), channel_id=1, source_target_pairs={{0,44},{4,48},{8,52},{12,56},{16,60},{20,32},{24,36},{28,40},{32,7... | collective-permute-start | bytes 147464 | tf_op jit(solution)/shard_map/ppermute | solution.py:69
  101.0 8.1 %collective-permute-start.7 = (bf16[3,8,1024]{2,1,0:T(8,128)(2,1)S(1)}, bf16[3,8,1024]{2,1,0:T(8,128)(2,1)S(1)}, u32[]{:S(2)}, u32[]{:S(2)}) collective-permute-start(bf16[3,8,1024]{2,1,0:T(8,128)(2,1)S(1)} %get-tuple-element.11), channel_id=1, source_target_pairs={{0,40},{4,44},{8,48},{12,52},{16,56},{20,60},{24,32},{28,36},{32,7... | collective-permute-start | bytes 147464 | tf_op jit(solution)/shard_map/ppermute | solution.py:69
  104.8 6.2 %collective-permute-start.8 = (bf16[3,8,1024]{2,1,0:T(8,128)(2,1)S(1)}, bf16[3,8,1024]{2,1,0:T(8,128)(2,1)S(1)}, u32[]{:S(2)}, u32[]{:S(2)}) collective-permute-start(bf16[3,8,1024]{2,1,0:T(8,128)(2,1)S(1)} %get-tuple-element.10), channel_id=1, source_target_pairs={{0,36},{4,40},{8,44},{12,48},{16,52},{20,56},{24,60},{28,32},{32,6... | collective-permute-start | bytes 147464 | tf_op jit(solution)/shard_map/ppermute | solution.py:69
  104.9 6.1 %collective-permute-start.9 = (bf16[3,8,1024]{2,1,0:T(8,128)(2,1)S(1)}, bf16[3,8,1024]{2,1,0:T(8,128)(2,1)S(1)}, u32[]{:S(2)}, u32[]{:S(2)}) collective-permute-start(bf16[3,8,1024]{2,1,0:T(8,128)(2,1)S(1)} %get-tuple-element.9), channel_id=1, source_target_pairs={{0,32},{4,36},{8,40},{12,44},{16,48},{20,52},{24,56},{28,60},{32,6... | collective-permute-start | bytes 147464 | tf_op jit(solution)/shard_map/ppermute | solution.py:69
  111.1 1.5 %copy-start.2 = (f32[128,128]{0,1:T(8,128)S(1)}, f32[128,128]{0,1:T(8,128)}, u32[]{:S(2)}) copy-start(f32[128,128]{0,1:T(8,128)} %constant.44.clone) | copy-start | bytes 196612
  111.2 1.5 %copy-start.3 = (f32[128,128]{0,1:T(8,128)S(1)}, f32[128,128]{0,1:T(8,128)}, u32[]{:S(2)}) copy-start(f32[128,128]{0,1:T(8,128)} %constant.45.clone) | copy-start | bytes 196612
  119.9 1.0 copy-start.7
  (3 other events, 2.6 us)
Sparse Core Ops, SparseCore 0:
  32.4 33.4 reduce-scatter.2
  68.4 28.4 reduce-scatter.4

commit v6 on v5

--- a/solution.py
+++ b/solution.py
@@ -58,6 +58,26 @@
     return lax.ppermute(value, axis, pairs)
 
 
+def ring_reduce_scatter(partial):
+    count = lax.axis_size("chan")
+    me = lax.axis_index("chan")
+    blocks = partial.reshape(count, partial.shape[0] // count, partial.shape[1])
+    half = partial.shape[1] // 2
+    right = [(i, (i + 1) % count) for i in range(count)]
+    left = [(i, (i - 1) % count) for i in range(count)]
+
+    def pick(index, lo):
+        block = lax.dynamic_index_in_dim(blocks, index % count, axis=0, keepdims=False)
+        return block[:, half:] if lo else block[:, :half]
+
+    ahead = pick(me - 1, False)
+    behind = pick(me + 1, True)
+    for step in range(2, count + 1):
+        ahead = lax.ppermute(ahead, "chan", right) + pick(me - step, False)
+        behind = lax.ppermute(behind, "chan", left) + pick(me + step, True)
+    return jnp.concatenate([ahead, behind], axis=1)
+
+
 def to_owner(value, shift):
     sections = lax.axis_size("section")
     count = lax.axis_size("seq")
@@ -101,7 +121,10 @@
         part = weight[:, :, :, chunk * shifts : (chunk + 1) * shifts].reshape(-1, 3 * n_chan * shifts * own)
         part = from_behind(part, "section", -1)
         partial = jnp.einsum("fn,rf->nr", part, rows, preferred_element_type=jnp.float32)
-        summed = lax.psum_scatter(partial, "chan", scatter_dimension=0, tiled=True)
+        if chunk == CHUNKS - 1:
+            summed = ring_reduce_scatter(partial)
+        else:
+            summed = lax.psum_scatter(partial, "chan", scatter_dimension=0, tiled=True)
         summed = summed.astype(jnp.bfloat16).reshape(3, shifts, own, seq_rows)
         for step in range(shifts):
             shift = chunk * shifts + step

time: 146 us -> 152 us (1.041)
  starting transfers between devices: 30.2 us -> 40.7 us
  waiting for transfers between devices: 54.4 us -> 44.8 us
  local copies, waits for them, and re-layouts: 8.24 us -> 12.6 us
    ppermute x2, waiting for transfers between devices: 35.9 us -> 1.97 us  [from_behind(): return lax.ppermute(value, axis, pairs)]
    ppermute x0 -> x6, waiting for transfers between devices: none -> 25.3 us  [the longest x3 19.4 us: ring_reduce_scatter(): behind = lax.ppermute(behind, 'chan', left) + pick(me + step, True)]
    ppermute x0 -> x6, starting transfers between devices: none -> 7.39 us  [the longest x3 7.14 us: ring_reduce_scatter(): behind = lax.ppermute(behind, 'chan', left) + pick(me + step, True)]
    ppermute x8, starting transfers between devices: 16.7 us -> 21.7 us  [to_owner(): return lax.ppermute(value, ('section', 'seq'), pairs)]
    convert_element_type x2, local copies, waits for them, and re-layouts: 0.23 us -> 2.85 us  [body(): queries = mixed[0].astype(jnp.float32)]
    slice x3, local copies, waits for them, and re-layouts: 0.49 us -> 2.89 us  [body(): weight[:, :, :, chunk * shifts:(chunk + 1) * shifts]]
    ppermute x2, starting transfers between devices: 1.93 us -> 0.3 us  [from_behind(): return lax.ppermute(value, axis, pairs)]
    unnamed x45 -> x43, local copies, waits for them, and re-layouts: 4.61 us -> 4.43 us
  transfers between devices with their start and end apart: 13 -> 18, of which waited for: 7 -> 12; matrix products, arithmetic and copies ran while one was open for 7% -> 10% of each run, Pallas kernels for 0% -> 0%
where the time goes in v6:
time: 152 us; the launch traced here: 151 us
  waiting for transfers between devices  44.8 us (29%)
  starting transfers between devices  40.7 us (27%)
  matrix products  19.2 us (13%)
  blocking collectives  16.6 us (11%)
  between operations  14 us (9%)
  local copies, waits for them, and re-layouts  12.6 us (8%)
  other arithmetic  3.19 us (2%)
    ppermute x8, starting transfers between devices, to_owner(): return lax.ppermute(value, ('section', 'seq'), pairs)  21.7 us
    ppermute x3, waiting for transfers between devices, ring_reduce_scatter(): behind = lax.ppermute(behind, 'chan', left) + pick(me + step, True)  19.4 us
    all_to_all x1, blocking collectives, body(): gated = lax.all_to_all(gated, ('seq', 'chan'), 0, 0, tiled=True)  16.6 us
    all_to_all x1, waiting for transfers between devices, body(): taps = lax.all_to_all(taps, ('seq', 'chan'), 0, 0, tiled=True)  12 us
    all_to_all x1, starting transfers between devices, body(): taps = lax.all_to_all(taps, ('seq', 'chan'), 0, 0, tiled=True)  11.3 us
    dot_general x2, matrix products, body(): jnp.einsum('fn,rf->nr', part, rows, preferred_element_type=jnp.float32)  8.93 us
    ppermute x3, starting transfers between devices, ring_reduce_scatter(): behind = lax.ppermute(behind, 'chan', left) + pick(me + step, True)  7.14 us
    ppermute x3, waiting for transfers between devices, ring_reduce_scatter(): ahead = lax.ppermute(ahead, 'chan', right) + pick(me - step, False)  5.91 us
  transfers between devices with their start and end apart: 18, of which 12 were waited for; matrix products, arithmetic and copies ran while one was open for 10% of the time, Pallas kernels for 0%

profile of v6, /device:TPU:8, one launch (start us, length us, event | category | flops | bytes accessed | tf_op | source)
XLA Modules:
  0.0 151.1 jit_solution(3171963992703978423)
XLA Ops:
  6.5 3.2 %copy.118 = bf16[1,2048,768]{1,2,0:T(8,128)(2,1)S(1)} copy(bf16[1,2048,768]{2,1,0:T(8,128)(2,1)} %param.13) | data formatting | bytes 6291456 | tf_op args[1]
  13.4 11.3 %all-to-all-start = ((f32[32,8,256]{2,1,0:T(8,128)}), f32[32,8,256]{2,1,0:T(8,128)S(1)}, u32[]{:S(2)}, u32[]{:S(2)}) async-start(f32[32,8,256]{2,1,0:T(8,128)} %bitcast.44), calls=%async_computation.1 | async-start | bytes 524288 | tf_op jit(solution)/shard_map/all_to_all | solution.py:109
  26.4 12.0 %all-to-all-done = f32[32,8,256]{2,1,0:T(8,128)S(1)} async-done(((f32[32,8,256]{2,1,0:T(8,128)}), f32[32,8,256]{2,1,0:T(8,128)S(1)}, u32[]{:S(2)}, u32[]{:S(2)}) %all-to-all-start) | async-done | bytes 262176 | tf_op jit(solution)/shard_map/all_to_all | solution.py:109
  41.2 4.4 %fusion.2 = f32[384,1024]{1,0:T(8,128)} fusion(bf16[2048,384]{0,1:T(8,128)(2,1)} %collective-permute-done.11, bf16[1,1024,2048]{2,1,0:T(8,128)(2,1)S(1)} %copy-done.12), kind=kOutput, calls=%fused_computation.4 | convolution fusion | flops 1610612736 | bytes 7340032 | tf_op jit(solution)/shard_map/fn,rf->nr/dot_general | solution.py:123
  45.7 2.0 %collective-permute-done = bf16[2048,384]{0,1:T(8,128)(2,1)} collective-permute-done((bf16[2048,384]{0,1:T(8,128)(2,1)}, bf16[2048,384]{0,1:T(8,128)(2,1)}, u32[]{:S(2)}, u32[]{:S(2)}) %collective-permute-start) | collective-permute-done | bytes 1572896 | tf_op jit(solution)/shard_map/ppermute | solution.py:58
  47.6 4.5 %fusion = f32[4,96,1024]{2,1,0:T(8,128)S(1)} fusion(bf16[4,96,2048]{2,1,0:T(8,128)(2,1)} %bitcast.4, bf16[1,1024,2048]{2,1,0:T(8,128)(2,1)} %param.12), kind=kOutput, calls=%fused_computation.2 | convolution fusion | flops 1610612736 | bytes 7340032 | tf_op jit(solution)/shard_map/fn,rf->nr/dot_general | solution.py:123
  52.4 2.8 %collective-permute-start.4 = (f32[96,512]{1,0:T(8,128)S(1)}, f32[96,512]{1,0:T(8,128)S(1)}, u32[]{:S(2)}, u32[]{:S(2)}) collective-permute-start(f32[96,512]{1,0:T(8,128)S(1)} %slice.92), channel_id=1, source_target_pairs={{0,3},{1,0},{2,1},{3,2},{4,7},{5,4},{6,5},{7,6},{8,11},{9,8},{10,9... | collective-permute-start | bytes 589832 | tf_op jit(solution)/shard_map/ppermute | solution.py:77
  55.7 8.6 %collective-permute-done.4 = f32[96,512]{1,0:T(8,128)S(1)} collective-permute-done((f32[96,512]{1,0:T(8,128)S(1)}, f32[96,512]{1,0:T(8,128)S(1)}, u32[]{:S(2)}, u32[]{:S(2)}) %collective-permute-start.4) | collective-permute-done | bytes 196640 | tf_op jit(solution)/shard_map/ppermute | solution.py:77
  64.4 2.5 %collective-permute-start.5 = (f32[96,512]{1,0:T(8,128)S(1)}, f32[96,512]{1,0:T(8,128)S(1)}, u32[]{:S(2)}, u32[]{:S(2)}) collective-permute-start(f32[96,512]{1,0:T(8,128)S(1)} %slice_add_fusion.2), channel_id=1, source_target_pairs={{0,3},{1,0},{2,1},{3,2},{4,7},{5,4},{6,5},{7,6},{8,11},{9,8},{10,9... | collective-permute-start | bytes 589832 | tf_op jit(solution)/shard_map/ppermute | solution.py:77
  66.8 2.0 %collective-permute-done.1 = f32[96,512]{1,0:T(8,128)S(1)} collective-permute-done((f32[96,512]{1,0:T(8,128)S(1)}, f32[96,512]{1,0:T(8,128)S(1)}, u32[]{:S(2)}, u32[]{:S(2)}) %collective-permute-start.1) | collective-permute-done | bytes 196640 | tf_op jit(solution)/shard_map/ppermute | solution.py:76
  69.0 6.2 %collective-permute-done.5 = f32[96,512]{1,0:T(8,128)S(1)} collective-permute-done((f32[96,512]{1,0:T(8,128)S(1)}, f32[96,512]{1,0:T(8,128)S(1)}, u32[]{:S(2)}, u32[]{:S(2)}) %collective-permute-start.5) | collective-permute-done | bytes 196640 | tf_op jit(solution)/shard_map/ppermute | solution.py:77
  75.2 1.8 %collective-permute-start.6 = (f32[96,512]{1,0:T(8,128)S(1)}, f32[96,512]{1,0:T(8,128)S(1)}, u32[]{:S(2)}, u32[]{:S(2)}) collective-permute-start(f32[96,512]{1,0:T(8,128)S(1)} %slice_add_fusion.1), channel_id=1, source_target_pairs={{0,3},{1,0},{2,1},{3,2},{4,7},{5,4},{6,5},{7,6},{8,11},{9,8},{10,9... | collective-permute-start | bytes 589832 | tf_op jit(solution)/shard_map/ppermute | solution.py:77
  77.8 4.6 %collective-permute-done.6 = f32[96,512]{1,0:T(8,128)S(1)} collective-permute-done((f32[96,512]{1,0:T(8,128)S(1)}, f32[96,512]{1,0:T(8,128)S(1)}, u32[]{:S(2)}, u32[]{:S(2)}) %collective-permute-start.6) | collective-permute-done | bytes 196640 | tf_op jit(solution)/shard_map/ppermute | solution.py:77
  82.4 3.2 %collective-permute-done.3 = f32[96,512]{1,0:T(8,128)S(1)} collective-permute-done((f32[96,512]{1,0:T(8,128)S(1)}, f32[96,512]{1,0:T(8,128)S(1)}, u32[]{:S(2)}, u32[]{:S(2)}) %collective-permute-start.3) | collective-permute-done | bytes 196640 | tf_op jit(solution)/shard_map/ppermute | solution.py:76
  85.7 4.3 %collective-permute-start.7 = (bf16[3,8,1024]{2,1,0:T(8,128)(2,1)S(1)}, bf16[3,8,1024]{2,1,0:T(8,128)(2,1)S(1)}, u32[]{:S(2)}, u32[]{:S(2)}) collective-permute-start(bf16[3,8,1024]{2,1,0:T(8,128)(2,1)S(1)} %get-tuple-element.22), channel_id=1, source_target_pairs={{0,60},{4,32},{8,36},{12,40},{16,44},{20,48},{24,52},{28,56},{32,9... | collective-permute-start | bytes 147464 | tf_op jit(solution)/shard_map/ppermute | solution.py:89
  90.4 4.2 %collective-permute-start.8 = (bf16[3,8,1024]{2,1,0:T(8,128)(2,1)S(1)}, bf16[3,8,1024]{2,1,0:T(8,128)(2,1)S(1)}, u32[]{:S(2)}, u32[]{:S(2)}) collective-permute-start(bf16[3,8,1024]{2,1,0:T(8,128)(2,1)S(1)} %get-tuple-element.23), channel_id=1, source_target_pairs={{0,56},{4,60},{8,32},{12,36},{16,40},{20,44},{24,48},{28,52},{32,8... | collective-permute-start | bytes 147464 | tf_op jit(solution)/shard_map/ppermute | solution.py:89
  95.1 5.6 %collective-permute-start.10 = (bf16[3,8,1024]{2,1,0:T(8,128)(2,1)S(1)}, bf16[3,8,1024]{2,1,0:T(8,128)(2,1)S(1)}, u32[]{:S(2)}, u32[]{:S(2)}) collective-permute-start(bf16[3,8,1024]{2,1,0:T(8,128)(2,1)S(1)} %get-tuple-element.21), channel_id=1, source_target_pairs={{0,48},{4,52},{8,56},{12,60},{16,32},{20,36},{24,40},{28,44},{32,8... | collective-permute-start | bytes 147464 | tf_op jit(solution)/shard_map/ppermute | solution.py:89
  104.1 2.9 %collective-permute-start.13 = (bf16[3,8,1024]{2,1,0:T(8,128)(2,1)S(1)}, bf16[3,8,1024]{2,1,0:T(8,128)(2,1)S(1)}, u32[]{:S(2)}, u32[]{:S(2)}) collective-permute-start(bf16[3,8,1024]{2,1,0:T(8,128)(2,1)S(1)} %get-tuple-element.19), channel_id=1, source_target_pairs={{0,40},{4,44},{8,48},{12,52},{16,56},{20,60},{24,32},{28,36},{32,7... | collective-permute-start | bytes 147464 | tf_op jit(solution)/shard_map/ppermute | solution.py:89
  107.0 3.4 %collective-permute-start.14 = (bf16[3,8,1024]{2,1,0:T(8,128)(2,1)S(1)}, bf16[3,8,1024]{2,1,0:T(8,128)(2,1)S(1)}, u32[]{:S(2)}, u32[]{:S(2)}) collective-permute-start(bf16[3,8,1024]{2,1,0:T(8,128)(2,1)S(1)} %get-tuple-element.18), channel_id=1, source_target_pairs={{0,36},{4,40},{8,44},{12,48},{16,52},{20,56},{24,60},{28,32},{32,6... | collective-permute-start | bytes 147464 | tf_op jit(solution)/shard_map/ppermute | solution.py:89
  110.8 3.6 %collective-permute-done.13 = bf16[3,8,1024]{2,1,0:T(8,128)(2,1)S(1)} collective-permute-done((bf16[3,8,1024]{2,1,0:T(8,128)(2,1)S(1)}, bf16[3,8,1024]{2,1,0:T(8,128)(2,1)S(1)}, u32[]{:S(2)}, u32[]{:S(2)}) %collective-permute-start.13) | collective-permute-done | bytes 49184 | tf_op jit(solution)/shard_map/ppermute | solution.py:89
  116.8 1.4 fusion.27
  118.9 1.8 %copy.128 = f32[1,8,8,1024]{3,2,1,0:T(8,128)} copy(f32[1,8,8,1024]{3,1,0,2:T(8,128)} %slice_convert_fusion) | data formatting | bytes 524288 | tf_op jit(solution)/shard_map/convert_element_type | solution.py:136
  121.7 1.6 %convolution_add_fusion.2 = f32[8,128,128]{2,1,0:T(8,128)S(1)} fusion(f32[8,128,128]{2,1,0:T(8,128)} %fusion.27, f32[128,128,1]{1,0,2:T(8,128)S(1)} %copy-done.4, f32[8,128,128]{1,2,0:T(8,128)S(1)} %convolution_bitcast_fusion, f32[8,128,128]{1,2,0:T(8,128)S(1)} %fusion.6, f32[128,128]{0,1:T(8,128)S(1)} %copy-done.2, f32[128,128]{0,1:T(8,128)S(1)} %copy-done.3), kind=kOutput, calls=%fused_computation.17 | convolution fusion | flops 101187584 | bytes 2293760 | tf_op jit(solution)/shard_map/ckr,rj->ckj/dot_general | solution.py:40
  126.9 16.6 %all_to_all.10 = bf16[32,8,256]{2,1,0:T(8,128)(2,1)S(1)} all-to-all(bf16[32,8,256]{2,1,0:T(8,128)(2,1)S(1)} %copy.146), channel_id=1, replica_groups=mesh['section'=8,'seq'=8,'chan'=4] {'seq','chan'}, dimensions={0} | all-to-all | bytes 262144 | tf_op jit(solution)/shard_map/all_to_all | solution.py:147
  (111 shorter events, 22.5 us)
Async XLA Ops:
  6.5 19.8 %copy-start = (f32[1,256]{1,0:T(1,128)S(1)}, f32[1,256]{1,0:T(1,128)}, u32[]{:S(2)}) copy-start(f32[1,256]{1,0:T(1,128)} %param.15) | copy-start | bytes 3076
  12.5 27.7 %collective-permute-start.11 = (bf16[2048,384]{0,1:T(8,128)(2,1)}, bf16[2048,384]{0,1:T(8,128)(2,1)}, u32[]{:S(2)}, u32[]{:S(2)}) collective-permute-start(bf16[2048,384]{0,1:T(8,128)(2,1)} %bitcast.25), channel_id=1, source_target_pairs={{0,224},{32,0},{64,32},{96,64},{128,96},{160,128},{192,160},{224,1... | collective-permute-start | bytes 4718600 | tf_op jit(solution)/shard_map/ppermute | solution.py:58
  13.4 25.0 %all-to-all-start = ((f32[32,8,256]{2,1,0:T(8,128)}), f32[32,8,256]{2,1,0:T(8,128)S(1)}, u32[]{:S(2)}, u32[]{:S(2)}) async-start(f32[32,8,256]{2,1,0:T(8,128)} %bitcast.44), calls=%async_computation.1 | async-start | bytes 524288 | tf_op jit(solution)/shard_map/all_to_all | solution.py:109
  24.7 77.4 %reduce-scatter.2.cloned.1.call-start = ((), (), s32[]{:S(2)}) async-start(), calls=%async_computation.3 | async-start | bytes 1966080 | tf_op jit(solution)/shard_map/reduce_scatter | solution.py:127
  24.8 13.8 %copy-start.9 = (f32[128,64,1]{0,1,2:T(8,128)S(1)}, f32[128,64,1]{0,1,2:T(8,128)}, u32[]{:S(2)}) copy-start(f32[128,64,1]{0,1,2:T(8,128)} %constant.124) | copy-start | bytes 98308
  26.0 12.9 %copy-start.8 = (f32[128,64,1]{0,1,2:T(8,128)S(1)}, f32[128,64,1]{0,1,2:T(8,128)}, u32[]{:S(2)}) copy-start(f32[128,64,1]{0,1,2:T(8,128)} %constant.123) | copy-start | bytes 98308
  26.1 13.4 %copy-start.1 = (f32[128,128,1]{1,0,2:T(8,128)S(1)}, f32[128,128,1]{1,0,2:T(8,128)}, u32[]{:S(2)}) copy-start(f32[128,128,1]{1,0,2:T(8,128)} %constant.125) | copy-start | bytes 196612
  26.1 13.4 %copy-start.5 = (f32[128,128]{1,0:T(8,128)S(1)}, f32[128,128]{1,0:T(8,128)}, u32[]{:S(2)}) copy-start(f32[128,128]{1,0:T(8,128)} %constant.128) | copy-start | bytes 196612
  26.1 13.4 %copy-start.6 = (f32[128,128]{1,0:T(8,128)S(1)}, f32[128,128]{1,0:T(8,128)}, u32[]{:S(2)}) copy-start(f32[128,128]{1,0:T(8,128)} %constant.127) | copy-start | bytes 196612
  26.1 21.6 %collective-permute-start = (bf16[2048,384]{0,1:T(8,128)(2,1)}, bf16[2048,384]{0,1:T(8,128)(2,1)}, u32[]{:S(2)}, u32[]{:S(2)}) collective-permute-start(bf16[2048,384]{0,1:T(8,128)(2,1)} %bitcast.2), channel_id=1, source_target_pairs={{0,224},{32,0},{64,32},{96,64},{128,96},{160,128},{192,160},{224,1... | collective-permute-start | bytes 4718600 | tf_op jit(solution)/shard_map/ppermute | solution.py:58
  52.4 11.9 %collective-permute-start.4 = (f32[96,512]{1,0:T(8,128)S(1)}, f32[96,512]{1,0:T(8,128)S(1)}, u32[]{:S(2)}, u32[]{:S(2)}) collective-permute-start(f32[96,512]{1,0:T(8,128)S(1)} %slice.92), channel_id=1, source_target_pairs={{0,3},{1,0},{2,1},{3,2},{4,7},{5,4},{6,5},{7,6},{8,11},{9,8},{10,9... | collective-permute-start | bytes 589832 | tf_op jit(solution)/shard_map/ppermute | solution.py:77
  55.6 13.2 %collective-permute-start.1 = (f32[96,512]{1,0:T(8,128)S(1)}, f32[96,512]{1,0:T(8,128)S(1)}, u32[]{:S(2)}, u32[]{:S(2)}) collective-permute-start(f32[96,512]{1,0:T(8,128)S(1)} %slice.88), channel_id=1, source_target_pairs={{0,1},{1,2},{2,3},{3,0},{4,5},{5,6},{6,7},{7,4},{8,9},{9,10},{10,1... | collective-permute-start | bytes 589832 | tf_op jit(solution)/shard_map/ppermute | solution.py:76
  64.4 10.8 %collective-permute-start.5 = (f32[96,512]{1,0:T(8,128)S(1)}, f32[96,512]{1,0:T(8,128)S(1)}, u32[]{:S(2)}, u32[]{:S(2)}) collective-permute-start(f32[96,512]{1,0:T(8,128)S(1)} %slice_add_fusion.2), channel_id=1, source_target_pairs={{0,3},{1,0},{2,1},{3,2},{4,7},{5,4},{6,5},{7,6},{8,11},{9,8},{10,9... | collective-permute-start | bytes 589832 | tf_op jit(solution)/shard_map/ppermute | solution.py:77
  68.9 8.8 %collective-permute-start.2 = (f32[96,512]{1,0:T(8,128)S(1)}, f32[96,512]{1,0:T(8,128)S(1)}, u32[]{:S(2)}, u32[]{:S(2)}) collective-permute-start(f32[96,512]{1,0:T(8,128)S(1)} %slice_add_fusion.5), channel_id=1, source_target_pairs={{0,1},{1,2},{2,3},{3,0},{4,5},{5,6},{6,7},{7,4},{8,9},{9,10},{10,1... | collective-permute-start | bytes 589832 | tf_op jit(solution)/shard_map/ppermute | solution.py:76
  75.2 7.2 %collective-permute-start.6 = (f32[96,512]{1,0:T(8,128)S(1)}, f32[96,512]{1,0:T(8,128)S(1)}, u32[]{:S(2)}, u32[]{:S(2)}) collective-permute-start(f32[96,512]{1,0:T(8,128)S(1)} %slice_add_fusion.1), channel_id=1, source_target_pairs={{0,3},{1,0},{2,1},{3,2},{4,7},{5,4},{6,5},{7,6},{8,11},{9,8},{10,9... | collective-permute-start | bytes 589832 | tf_op jit(solution)/shard_map/ppermute | solution.py:77
  77.7 7.9 %collective-permute-start.3 = (f32[96,512]{1,0:T(8,128)S(1)}, f32[96,512]{1,0:T(8,128)S(1)}, u32[]{:S(2)}, u32[]{:S(2)}) collective-permute-start(f32[96,512]{1,0:T(8,128)S(1)} %slice_add_fusion.4), channel_id=1, source_target_pairs={{0,1},{1,2},{2,3},{3,0},{4,5},{5,6},{6,7},{7,4},{8,9},{9,10},{10,1... | collective-permute-start | bytes 589832 | tf_op jit(solution)/shard_map/ppermute | solution.py:76
  85.7 15.0 %collective-permute-start.7 = (bf16[3,8,1024]{2,1,0:T(8,128)(2,1)S(1)}, bf16[3,8,1024]{2,1,0:T(8,128)(2,1)S(1)}, u32[]{:S(2)}, u32[]{:S(2)}) collective-permute-start(bf16[3,8,1024]{2,1,0:T(8,128)(2,1)S(1)} %get-tuple-element.22), channel_id=1, source_target_pairs={{0,60},{4,32},{8,36},{12,40},{16,44},{20,48},{24,52},{28,56},{32,9... | collective-permute-start | bytes 147464 | tf_op jit(solution)/shard_map/ppermute | solution.py:89
  90.4 10.3 %collective-permute-start.8 = (bf16[3,8,1024]{2,1,0:T(8,128)(2,1)S(1)}, bf16[3,8,1024]{2,1,0:T(8,128)(2,1)S(1)}, u32[]{:S(2)}, u32[]{:S(2)}) collective-permute-start(bf16[3,8,1024]{2,1,0:T(8,128)(2,1)S(1)} %get-tuple-element.23), channel_id=1, source_target_pairs={{0,56},{4,60},{8,32},{12,36},{16,40},{20,44},{24,48},{28,52},{32,8... | collective-permute-start | bytes 147464 | tf_op jit(solution)/shard_map/ppermute | solution.py:89
  94.6 7.5 %collective-permute-start.9 = (bf16[3,8,1024]{2,1,0:T(8,128)(2,1)S(1)}, bf16[3,8,1024]{2,1,0:T(8,128)(2,1)S(1)}, u32[]{:S(2)}, u32[]{:S(2)}) collective-permute-start(bf16[3,8,1024]{2,1,0:T(8,128)(2,1)S(1)} %get-tuple-element.24), channel_id=1, source_target_pairs={{0,52},{4,56},{8,60},{12,32},{16,36},{20,40},{24,44},{28,48},{32,8... | collective-permute-start | bytes 147464 | tf_op jit(solution)/shard_map/ppermute | solution.py:89
  95.1 9.0 %collective-permute-start.10 = (bf16[3,8,1024]{2,1,0:T(8,128)(2,1)S(1)}, bf16[3,8,1024]{2,1,0:T(8,128)(2,1)S(1)}, u32[]{:S(2)}, u32[]{:S(2)}) collective-permute-start(bf16[3,8,1024]{2,1,0:T(8,128)(2,1)S(1)} %get-tuple-element.21), channel_id=1, source_target_pairs={{0,48},{4,52},{8,56},{12,60},{16,32},{20,36},{24,40},{28,44},{32,8... | collective-permute-start | bytes 147464 | tf_op jit(solution)/shard_map/ppermute | solution.py:89
  103.2 7.6 %collective-permute-start.12 = (bf16[3,8,1024]{2,1,0:T(8,128)(2,1)S(1)}, bf16[3,8,1024]{2,1,0:T(8,128)(2,1)S(1)}, u32[]{:S(2)}, u32[]{:S(2)}) collective-permute-start(bf16[3,8,1024]{2,1,0:T(8,128)(2,1)S(1)} %get-tuple-element.20), channel_id=1, source_target_pairs={{0,44},{4,48},{8,52},{12,56},{16,60},{20,32},{24,36},{28,40},{32,7... | collective-permute-start | bytes 147464 | tf_op jit(solution)/shard_map/ppermute | solution.py:89
  104.1 10.3 %collective-permute-start.13 = (bf16[3,8,1024]{2,1,0:T(8,128)(2,1)S(1)}, bf16[3,8,1024]{2,1,0:T(8,128)(2,1)S(1)}, u32[]{:S(2)}, u32[]{:S(2)}) collective-permute-start(bf16[3,8,1024]{2,1,0:T(8,128)(2,1)S(1)} %get-tuple-element.19), channel_id=1, source_target_pairs={{0,40},{4,44},{8,48},{12,52},{16,56},{20,60},{24,32},{28,36},{32,7... | collective-permute-start | bytes 147464 | tf_op jit(solution)/shard_map/ppermute | solution.py:89
  107.0 7.5 %collective-permute-start.14 = (bf16[3,8,1024]{2,1,0:T(8,128)(2,1)S(1)}, bf16[3,8,1024]{2,1,0:T(8,128)(2,1)S(1)}, u32[]{:S(2)}, u32[]{:S(2)}) collective-permute-start(bf16[3,8,1024]{2,1,0:T(8,128)(2,1)S(1)} %get-tuple-element.18), channel_id=1, source_target_pairs={{0,36},{4,40},{8,44},{12,48},{16,52},{20,56},{24,60},{28,32},{32,6... | collective-permute-start | bytes 147464 | tf_op jit(solution)/shard_map/ppermute | solution.py:89
  110.4 4.0 %collective-permute-start.15 = (bf16[3,8,1024]{2,1,0:T(8,128)(2,1)S(1)}, bf16[3,8,1024]{2,1,0:T(8,128)(2,1)S(1)}, u32[]{:S(2)}, u32[]{:S(2)}) collective-permute-start(bf16[3,8,1024]{2,1,0:T(8,128)(2,1)S(1)} %get-tuple-element.17), channel_id=1, source_target_pairs={{0,32},{4,36},{8,40},{12,44},{16,48},{20,52},{24,56},{28,60},{32,6... | collective-permute-start | bytes 147464 | tf_op jit(solution)/shard_map/ppermute | solution.py:89
  (7 other events, 9.6 us)
Sparse Core Ops, SparseCore 0:
  45.8 29.4 reduce-scatter.1

commit v7 on v5

--- a/solution.py
+++ b/solution.py
@@ -58,6 +58,13 @@
     return lax.ppermute(value, axis, pairs)
 
 
+def exchange_sum(partial):
+    count = lax.axis_size("chan")
+    blocks = partial.reshape(count, partial.shape[0] // count, partial.shape[1])
+    blocks = lax.all_to_all(blocks, "chan", 0, 0, tiled=True)
+    return jnp.sum(blocks, axis=0)
+
+
 def to_owner(value, shift):
     sections = lax.axis_size("section")
     count = lax.axis_size("seq")
@@ -101,7 +108,7 @@
         part = weight[:, :, :, chunk * shifts : (chunk + 1) * shifts].reshape(-1, 3 * n_chan * shifts * own)
         part = from_behind(part, "section", -1)
         partial = jnp.einsum("fn,rf->nr", part, rows, preferred_element_type=jnp.float32)
-        summed = lax.psum_scatter(partial, "chan", scatter_dimension=0, tiled=True)
+        summed = exchange_sum(partial)
         summed = summed.astype(jnp.bfloat16).reshape(3, shifts, own, seq_rows)
         for step in range(shifts):
             shift = chunk * shifts + step

time: 146 us -> 124 us (0.85)
  waiting for transfers between devices: 54.4 us -> 30.7 us
  between operations: 14 us -> 0.57 us
  starting transfers between devices: 30.2 us -> 42.4 us
  matrix products: 18.6 us -> 20.5 us
    ppermute x2, waiting for transfers between devices: 35.9 us -> 6.89 us  [from_behind(): return lax.ppermute(value, axis, pairs)]
    all_to_all x0 -> x2, waiting for transfers between devices: none -> 15.8 us  [exchange_sum(): blocks = lax.all_to_all(blocks, 'chan', 0, 0, tiled=True)]
    all_to_all x1, waiting for transfers between devices: 12.7 us -> 3.53 us  [body(): taps = lax.all_to_all(taps, ('seq', 'chan'), 0, 0, tiled=True)]
    all_to_all x0 -> x2, starting transfers between devices: none -> 7.92 us  [exchange_sum(): blocks = lax.all_to_all(blocks, 'chan', 0, 0, tiled=True)]
    ppermute x8, starting transfers between devices: 16.7 us -> 22.6 us  [to_owner(): return lax.ppermute(value, ('section', 'seq'), pairs)]
    dot_general x2, matrix products: 8.18 us -> 11.3 us  [body(): jnp.einsum('fn,rf->nr', part, rows, preferred_element_type=jnp.float32)]
    convert_element_type x2 -> x0, other arithmetic: 2.04 us -> none  [body(): summed = summed.astype(jnp.bfloat16).reshape(3, shifts, own, seq_rows)]
    all_to_all x1, starting transfers between devices: 11.5 us -> 9.61 us  [body(): taps = lax.all_to_all(taps, ('seq', 'chan'), 0, 0, tiled=True)]
  transfers between devices with their start and end apart: 13 -> 13, of which waited for: 7 -> 7; matrix products, arithmetic and copies ran while one was open for 7% -> 15% of each run, Pallas kernels for 0% -> 0%
where the time goes in v7:
time: 124 us; the launch traced here: 122 us
  starting transfers between devices  42.4 us (34%)
  waiting for transfers between devices  30.7 us (25%)
  matrix products  20.5 us (17%)
  blocking collectives  15.8 us (13%)
  local copies, waits for them, and re-layouts  9.34 us (8%)
  other arithmetic  2.96 us (2%)
    ppermute x8, starting transfers between devices, to_owner(): return lax.ppermute(value, ('section', 'seq'), pairs)  22.6 us
    all_to_all x2, waiting for transfers between devices, exchange_sum(): blocks = lax.all_to_all(blocks, 'chan', 0, 0, tiled=True)  15.8 us
    all_to_all x1, blocking collectives, body(): gated = lax.all_to_all(gated, ('seq', 'chan'), 0, 0, tiled=True)  15.8 us
    dot_general x2, matrix products, body(): jnp.einsum('fn,rf->nr', part, rows, preferred_element_type=jnp.float32)  11.3 us
    all_to_all x1, starting transfers between devices, body(): taps = lax.all_to_all(taps, ('seq', 'chan'), 0, 0, tiled=True)  9.61 us
    all_to_all x2, starting transfers between devices, exchange_sum(): blocks = lax.all_to_all(blocks, 'chan', 0, 0, tiled=True)  7.92 us
    ppermute x2, waiting for transfers between devices, from_behind(): return lax.ppermute(value, axis, pairs)  6.89 us
    unnamed x49, local copies, waits for them, and re-layouts  4.55 us
  transfers between devices with their start and end apart: 13, of which 7 were waited for; matrix products, arithmetic and copies ran while one was open for 15% of the time, Pallas kernels for 0%

profile of v7, /device:TPU:8, one launch (start us, length us, event | category | flops | bytes accessed | tf_op | source)
XLA Modules:
  0.0 122.3 jit_solution(14490408235669574748)
XLA Ops:
  0.0 3.2 %copy.90 = bf16[1,2048,768]{1,2,0:T(8,128)(2,1)S(1)} copy(bf16[1,2048,768]{2,1,0:T(8,128)(2,1)} %param.13) | data formatting | bytes 6291456 | tf_op args[1]
  3.2 1.1 fusion.5
  4.7 1.4 %copy.94 = bf16[2048,4,3,4,8]{0,4,3,2,1:T(8,128)(2,1)} copy(bf16[2048,4,3,4,8]{0,4,3,1,2:T(8,128)(2,1)S(1)} %get-tuple-element.5) | data formatting | bytes 3145728 | tf_op jit(solution)/shard_map/slice | solution.py:108
  6.1 2.2 %collective-permute-start.5 = (bf16[2048,384]{0,1:T(8,128)(2,1)}, bf16[2048,384]{0,1:T(8,128)(2,1)}, u32[]{:S(2)}, u32[]{:S(2)}) collective-permute-start(bf16[2048,384]{0,1:T(8,128)(2,1)} %bitcast.16), channel_id=1, source_target_pairs={{0,224},{32,0},{64,32},{96,64},{128,96},{160,128},{192,160},{224,1... | collective-permute-start | bytes 4718600 | tf_op jit(solution)/shard_map/ppermute | solution.py:58
  9.2 9.6 %all-to-all-start.2 = ((f32[32,8,256]{2,1,0:T(8,128)}), f32[32,8,256]{2,1,0:T(8,128)S(1)}, u32[]{:S(2)}, u32[]{:S(2)}) async-start(f32[32,8,256]{2,1,0:T(8,128)} %bitcast.37), calls=%async_computation.2 | async-start | bytes 524288 | tf_op jit(solution)/shard_map/all_to_all | solution.py:96
  18.8 3.8 %collective-permute-done = bf16[2048,384]{0,1:T(8,128)(2,1)} collective-permute-done((bf16[2048,384]{0,1:T(8,128)(2,1)S(1)}, bf16[2048,384]{0,1:T(8,128)(2,1)}, u32[]{:S(2)}, u32[]{:S(2)}) %collective-permute-start) | collective-permute-done | bytes 1572896 | tf_op jit(solution)/shard_map/ppermute | solution.py:58
  22.6 5.6 %fusion.2 = f32[4,96,1024]{2,1,0:T(8,128)} fusion(bf16[4,96,2048]{2,1,0:T(8,128)(2,1)} %bitcast.4, bf16[1,1024,2048]{2,1,0:T(8,128)(2,1)} %param.12), kind=kOutput, calls=%fused_computation.4 | convolution fusion | flops 1610612736 | bytes 7340032 | tf_op jit(solution)/shard_map/fn,rf->nr/dot_general | solution.py:110
  28.3 3.5 %all-to-all-done.2 = f32[32,8,256]{2,1,0:T(8,128)S(1)} async-done(((f32[32,8,256]{2,1,0:T(8,128)}), f32[32,8,256]{2,1,0:T(8,128)S(1)}, u32[]{:S(2)}, u32[]{:S(2)}) %all-to-all-start.2) | async-done | bytes 262176 | tf_op jit(solution)/shard_map/all_to_all | solution.py:96
  31.8 3.6 %all-to-all-start = ((f32[4,96,1024]{2,1,0:T(8,128)}), f32[4,96,1024]{2,1,0:T(8,128)S(1)}, u32[]{:S(2)}, u32[]{:S(2)}) async-start(f32[4,96,1024]{2,1,0:T(8,128)} %fusion.2), calls=%async_computation | async-start | bytes 3145728 | tf_op jit(solution)/shard_map/all_to_all | solution.py:64
  36.5 3.1 %collective-permute-done.5 = bf16[2048,384]{0,1:T(8,128)(2,1)} collective-permute-done((bf16[2048,384]{0,1:T(8,128)(2,1)}, bf16[2048,384]{0,1:T(8,128)(2,1)}, u32[]{:S(2)}, u32[]{:S(2)}) %collective-permute-start.5) | collective-permute-done | bytes 1572896 | tf_op jit(solution)/shard_map/ppermute | solution.py:58
  39.6 5.7 %fusion = f32[4,96,1024]{2,1,0:T(8,128)} fusion(bf16[4,96,2048]{2,1,0:T(8,128)(2,1)} %bitcast.18, bf16[1,1024,2048]{2,1,0:T(8,128)(2,1)} %param.12), kind=kOutput, calls=%fused_computation.2 | convolution fusion | flops 1610612736 | bytes 7340032 | tf_op jit(solution)/shard_map/fn,rf->nr/dot_general | solution.py:110
  45.3 10.5 %all-to-all-done = f32[4,96,1024]{2,1,0:T(8,128)S(1)} async-done(((f32[4,96,1024]{2,1,0:T(8,128)}), f32[4,96,1024]{2,1,0:T(8,128)S(1)}, u32[]{:S(2)}, u32[]{:S(2)}) %all-to-all-start) | async-done | bytes 1572896 | tf_op jit(solution)/shard_map/all_to_all | solution.py:64
  55.7 4.4 %all-to-all-start.1 = ((f32[4,96,1024]{2,1,0:T(8,128)}), f32[4,96,1024]{2,1,0:T(8,128)}, u32[]{:S(2)}, u32[]{:S(2)}) async-start(f32[4,96,1024]{2,1,0:T(8,128)} %fusion), calls=%async_computation.1 | async-start | bytes 3145728 | tf_op jit(solution)/shard_map/all_to_all | solution.py:64
  61.3 1.2 convolution_subtract_fusion.1
  62.7 4.5 %collective-permute-start.1 = (bf16[3,8,1024]{2,1,0:T(8,128)(2,1)S(1)}, bf16[3,8,1024]{2,1,0:T(8,128)(2,1)S(1)}, u32[]{:S(2)}, u32[]{:S(2)}) collective-permute-start(bf16[3,8,1024]{2,1,0:T(8,128)(2,1)S(1)} %get-tuple-element.14), channel_id=1, source_target_pairs={{0,60},{4,32},{8,36},{12,40},{16,44},{20,48},{24,52},{28,56},{32,9... | collective-permute-start | bytes 147464 | tf_op jit(solution)/shard_map/ppermute | solution.py:76
  67.1 2.0 %collective-permute-start.2 = (bf16[3,8,1024]{2,1,0:T(8,128)(2,1)S(1)}, bf16[3,8,1024]{2,1,0:T(8,128)(2,1)S(1)}, u32[]{:S(2)}, u32[]{:S(2)}) collective-permute-start(bf16[3,8,1024]{2,1,0:T(8,128)(2,1)S(1)} %get-tuple-element.16), channel_id=1, source_target_pairs={{0,56},{4,60},{8,32},{12,36},{16,40},{20,44},{24,48},{28,52},{32,8... | collective-permute-start | bytes 147464 | tf_op jit(solution)/shard_map/ppermute | solution.py:76
  69.1 1.0 collective-permute-start.3
  70.1 4.3 %collective-permute-start.4 = (bf16[3,8,1024]{2,1,0:T(8,128)(2,1)S(1)}, bf16[3,8,1024]{2,1,0:T(8,128)(2,1)S(1)}, u32[]{:S(2)}, u32[]{:S(2)}) collective-permute-start(bf16[3,8,1024]{2,1,0:T(8,128)(2,1)S(1)} %get-tuple-element.13), channel_id=1, source_target_pairs={{0,48},{4,52},{8,56},{12,60},{16,32},{20,36},{24,40},{28,44},{32,8... | collective-permute-start | bytes 147464 | tf_op jit(solution)/shard_map/ppermute | solution.py:76
  74.3 5.3 %all-to-all-done.1 = f32[4,96,1024]{2,1,0:T(8,128)} async-done(((f32[4,96,1024]{2,1,0:T(8,128)}), f32[4,96,1024]{2,1,0:T(8,128)}, u32[]{:S(2)}, u32[]{:S(2)}) %all-to-all-start.1) | async-done | bytes 1572896 | tf_op jit(solution)/shard_map/all_to_all | solution.py:64
  79.7 1.6 %reduce_sum.19 = bf16[96,1024]{1,0:T(8,128)(2,1)S(1)} reduce(f32[4,96,1024]{2,1,0:T(8,128)} %all-to-all-done.1, f32[]{:T(128)} %constant.17.clone.1), dimensions={0}, to_apply=%region_1.0 | reduce | flops 294912 | bytes 1769476 | tf_op jit(solution)/shard_map/reduce_sum | solution.py:65
  81.3 4.9 %collective-permute-start.6 = (bf16[3,8,1024]{2,1,0:T(8,128)(2,1)S(1)}, bf16[3,8,1024]{2,1,0:T(8,128)(2,1)S(1)}, u32[]{:S(2)}, u32[]{:S(2)}) collective-permute-start(bf16[3,8,1024]{2,1,0:T(8,128)(2,1)S(1)} %get-tuple-element.11), channel_id=1, source_target_pairs={{0,44},{4,48},{8,52},{12,56},{16,60},{20,32},{24,36},{28,40},{32,7... | collective-permute-start | bytes 147464 | tf_op jit(solution)/shard_map/ppermute | solution.py:76
  86.2 4.8 %collective-permute-start.7 = (bf16[3,8,1024]{2,1,0:T(8,128)(2,1)S(1)}, bf16[3,8,1024]{2,1,0:T(8,128)(2,1)S(1)}, u32[]{:S(2)}, u32[]{:S(2)}) collective-permute-start(bf16[3,8,1024]{2,1,0:T(8,128)(2,1)S(1)} %get-tuple-element.10), channel_id=1, source_target_pairs={{0,40},{4,44},{8,48},{12,52},{16,56},{20,60},{24,32},{28,36},{32,7... | collective-permute-start | bytes 147464 | tf_op jit(solution)/shard_map/ppermute | solution.py:76
  92.9 3.8 %collective-permute-done.8 = bf16[3,8,1024]{2,1,0:T(8,128)(2,1)S(1)} collective-permute-done((bf16[3,8,1024]{2,1,0:T(8,128)(2,1)S(1)}, bf16[3,8,1024]{2,1,0:T(8,128)(2,1)S(1)}, u32[]{:S(2)}, u32[]{:S(2)}) %collective-permute-start.8) | collective-permute-done | bytes 49184 | tf_op jit(solution)/shard_map/ppermute | solution.py:76
  105.7 15.8 %all_to_all.20 = bf16[32,8,256]{2,1,0:T(8,128)(2,1)S(1)} all-to-all(bf16[32,8,256]{2,1,0:T(8,128)(2,1)S(1)} %copy.116), channel_id=1, replica_groups=mesh['section'=8,'seq'=8,'chan'=4] {'seq','chan'}, dimensions={0} | all-to-all | bytes 262144 | tf_op jit(solution)/shard_map/all_to_all | solution.py:131
  (98 shorter events, 15.0 us)
Async XLA Ops:
  0.0 35.4 %copy-start = (f32[1,256]{1,0:T(1,128)S(1)}, f32[1,256]{1,0:T(1,128)}, u32[]{:S(2)}) copy-start(f32[1,256]{1,0:T(1,128)} %param.15) | copy-start | bytes 3076
  4.7 18.0 %collective-permute-start = (bf16[2048,384]{0,1:T(8,128)(2,1)S(1)}, bf16[2048,384]{0,1:T(8,128)(2,1)}, u32[]{:S(2)}, u32[]{:S(2)}) collective-permute-start(bf16[2048,384]{0,1:T(8,128)(2,1)S(1)} %bitcast.141), channel_id=1, source_target_pairs={{0,224},{32,0},{64,32},{96,64},{128,96},{160,128},{192,160},{224,1... | collective-permute-start | bytes 4718600 | tf_op jit(solution)/shard_map/ppermute | solution.py:58
  4.7 3.6 %copy-start.9 = (f32[1,256,256]{2,1,0:T(8,128)S(1)}, f32[1,256,256]{2,1,0:T(8,128)}, u32[]{:S(2)}) copy-start(f32[1,256,256]{2,1,0:T(8,128)} %param.14) | copy-start | bytes 786436
  6.1 33.5 %collective-permute-start.5 = (bf16[2048,384]{0,1:T(8,128)(2,1)}, bf16[2048,384]{0,1:T(8,128)(2,1)}, u32[]{:S(2)}, u32[]{:S(2)}) collective-permute-start(bf16[2048,384]{0,1:T(8,128)(2,1)} %bitcast.16), channel_id=1, source_target_pairs={{0,224},{32,0},{64,32},{96,64},{128,96},{160,128},{192,160},{224,1... | collective-permute-start | bytes 4718600 | tf_op jit(solution)/shard_map/ppermute | solution.py:58
  9.2 22.6 %all-to-all-start.2 = ((f32[32,8,256]{2,1,0:T(8,128)}), f32[32,8,256]{2,1,0:T(8,128)S(1)}, u32[]{:S(2)}, u32[]{:S(2)}) async-start(f32[32,8,256]{2,1,0:T(8,128)} %bitcast.37), calls=%async_computation.2 | async-start | bytes 524288 | tf_op jit(solution)/shard_map/all_to_all | solution.py:96
  28.3 7.3 %copy-start.10 = (f32[128,64,1]{0,1,2:T(8,128)S(1)}, f32[128,64,1]{0,1,2:T(8,128)}, u32[]{:S(2)}) copy-start(f32[128,64,1]{0,1,2:T(8,128)} %constant.55) | copy-start | bytes 98308
  31.8 23.9 %all-to-all-start = ((f32[4,96,1024]{2,1,0:T(8,128)}), f32[4,96,1024]{2,1,0:T(8,128)S(1)}, u32[]{:S(2)}, u32[]{:S(2)}) async-start(f32[4,96,1024]{2,1,0:T(8,128)} %fusion.2), calls=%async_computation | async-start | bytes 3145728 | tf_op jit(solution)/shard_map/all_to_all | solution.py:64
  45.3 14.8 %copy-start.1 = (f32[128,128,1]{1,0,2:T(8,128)S(1)}, f32[128,128,1]{1,0,2:T(8,128)}, u32[]{:S(2)}) copy-start(f32[128,128,1]{1,0,2:T(8,128)} %constant.56) | copy-start | bytes 196612
  45.3 14.8 %copy-start.6 = (f32[128,128]{1,0:T(8,128)S(1)}, f32[128,128]{1,0:T(8,128)}, u32[]{:S(2)}) copy-start(f32[128,128]{1,0:T(8,128)} %constant.58) | copy-start | bytes 196612
  45.3 14.8 %copy-start.7 = (f32[128,128]{1,0:T(8,128)S(1)}, f32[128,128]{1,0:T(8,128)}, u32[]{:S(2)}) copy-start(f32[128,128]{1,0:T(8,128)} %constant.59) | copy-start | bytes 196612
  55.7 24.0 %all-to-all-start.1 = ((f32[4,96,1024]{2,1,0:T(8,128)}), f32[4,96,1024]{2,1,0:T(8,128)}, u32[]{:S(2)}, u32[]{:S(2)}) async-start(f32[4,96,1024]{2,1,0:T(8,128)} %fusion), calls=%async_computation.1 | async-start | bytes 3145728 | tf_op jit(solution)/shard_map/all_to_all | solution.py:64
  62.7 23.5 %collective-permute-start.1 = (bf16[3,8,1024]{2,1,0:T(8,128)(2,1)S(1)}, bf16[3,8,1024]{2,1,0:T(8,128)(2,1)S(1)}, u32[]{:S(2)}, u32[]{:S(2)}) collective-permute-start(bf16[3,8,1024]{2,1,0:T(8,128)(2,1)S(1)} %get-tuple-element.14), channel_id=1, source_target_pairs={{0,60},{4,32},{8,36},{12,40},{16,44},{20,48},{24,52},{28,56},{32,9... | collective-permute-start | bytes 147464 | tf_op jit(solution)/shard_map/ppermute | solution.py:76
  67.1 23.9 %collective-permute-start.2 = (bf16[3,8,1024]{2,1,0:T(8,128)(2,1)S(1)}, bf16[3,8,1024]{2,1,0:T(8,128)(2,1)S(1)}, u32[]{:S(2)}, u32[]{:S(2)}) collective-permute-start(bf16[3,8,1024]{2,1,0:T(8,128)(2,1)S(1)} %get-tuple-element.16), channel_id=1, source_target_pairs={{0,56},{4,60},{8,32},{12,36},{16,40},{20,44},{24,48},{28,52},{32,8... | collective-permute-start | bytes 147464 | tf_op jit(solution)/shard_map/ppermute | solution.py:76
  69.1 22.4 %collective-permute-start.3 = (bf16[3,8,1024]{2,1,0:T(8,128)(2,1)S(1)}, bf16[3,8,1024]{2,1,0:T(8,128)(2,1)S(1)}, u32[]{:S(2)}, u32[]{:S(2)}) collective-permute-start(bf16[3,8,1024]{2,1,0:T(8,128)(2,1)S(1)} %get-tuple-element.15), channel_id=1, source_target_pairs={{0,52},{4,56},{8,60},{12,32},{16,36},{20,40},{24,44},{28,48},{32,8... | collective-permute-start | bytes 147464 | tf_op jit(solution)/shard_map/ppermute | solution.py:76
  70.1 22.1 %collective-permute-start.4 = (bf16[3,8,1024]{2,1,0:T(8,128)(2,1)S(1)}, bf16[3,8,1024]{2,1,0:T(8,128)(2,1)S(1)}, u32[]{:S(2)}, u32[]{:S(2)}) collective-permute-start(bf16[3,8,1024]{2,1,0:T(8,128)(2,1)S(1)} %get-tuple-element.13), channel_id=1, source_target_pairs={{0,48},{4,52},{8,56},{12,60},{16,32},{20,36},{24,40},{28,44},{32,8... | collective-permute-start | bytes 147464 | tf_op jit(solution)/shard_map/ppermute | solution.py:76
  81.3 10.9 %collective-permute-start.6 = (bf16[3,8,1024]{2,1,0:T(8,128)(2,1)S(1)}, bf16[3,8,1024]{2,1,0:T(8,128)(2,1)S(1)}, u32[]{:S(2)}, u32[]{:S(2)}) collective-permute-start(bf16[3,8,1024]{2,1,0:T(8,128)(2,1)S(1)} %get-tuple-element.11), channel_id=1, source_target_pairs={{0,44},{4,48},{8,52},{12,56},{16,60},{20,32},{24,36},{28,40},{32,7... | collective-permute-start | bytes 147464 | tf_op jit(solution)/shard_map/ppermute | solution.py:76
  86.2 6.7 %collective-permute-start.7 = (bf16[3,8,1024]{2,1,0:T(8,128)(2,1)S(1)}, bf16[3,8,1024]{2,1,0:T(8,128)(2,1)S(1)}, u32[]{:S(2)}, u32[]{:S(2)}) collective-permute-start(bf16[3,8,1024]{2,1,0:T(8,128)(2,1)S(1)} %get-tuple-element.10), channel_id=1, source_target_pairs={{0,40},{4,44},{8,48},{12,52},{16,56},{20,60},{24,32},{28,36},{32,7... | collective-permute-start | bytes 147464 | tf_op jit(solution)/shard_map/ppermute | solution.py:76
  91.0 5.7 %collective-permute-start.8 = (bf16[3,8,1024]{2,1,0:T(8,128)(2,1)S(1)}, bf16[3,8,1024]{2,1,0:T(8,128)(2,1)S(1)}, u32[]{:S(2)}, u32[]{:S(2)}) collective-permute-start(bf16[3,8,1024]{2,1,0:T(8,128)(2,1)S(1)} %get-tuple-element.12), channel_id=1, source_target_pairs={{0,36},{4,40},{8,44},{12,48},{16,52},{20,56},{24,60},{28,32},{32,6... | collective-permute-start | bytes 147464 | tf_op jit(solution)/shard_map/ppermute | solution.py:76
  91.5 5.3 %collective-permute-start.9 = (bf16[3,8,1024]{2,1,0:T(8,128)(2,1)S(1)}, bf16[3,8,1024]{2,1,0:T(8,128)(2,1)S(1)}, u32[]{:S(2)}, u32[]{:S(2)}) collective-permute-start(bf16[3,8,1024]{2,1,0:T(8,128)(2,1)S(1)} %get-tuple-element.9), channel_id=1, source_target_pairs={{0,32},{4,36},{8,40},{12,44},{16,48},{20,52},{24,56},{28,60},{32,6... | collective-permute-start | bytes 147464 | tf_op jit(solution)/shard_map/ppermute | solution.py:76
  96.9 1.2 %copy-start.11 = (f32[128,64,1]{0,1,2:T(8,128)S(1)}, f32[128,64,1]{0,1,2:T(8,128)}, u32[]{:S(2)}) copy-start(f32[128,64,1]{0,1,2:T(8,128)} %constant.55) | copy-start | bytes 98308
  96.9 1.8 %copy-start.2 = (f32[128,128]{0,1:T(8,128)S(1)}, f32[128,128]{0,1:T(8,128)}, u32[]{:S(2)}) copy-start(f32[128,128]{0,1:T(8,128)} %constant.46.clone) | copy-start | bytes 196612
  96.9 1.8 %copy-start.3 = (f32[128,128]{0,1:T(8,128)S(1)}, f32[128,128]{0,1:T(8,128)}, u32[]{:S(2)}) copy-start(f32[128,128]{0,1:T(8,128)} %constant.47.clone) | copy-start | bytes 196612
  100.7 1.0 copy-start.5
  104.6 1.0 copy-start.8
  (5 other events, 4.1 us)
